TPU v7x, 256 devices: a whole 4x4x8 slice. The times are simulated.
256 devices in a mesh: wide: 32 (over z, y), narrow: 8 (over x, core).
Axes of the slice: x: 4, y: 4, z: 8, core: 2. Of those that a mesh axis runs over, the one named last changes fastest.
Arguments:
- hidden: bfloat16 [65536, 8192], P('wide', 'narrow'), may hold values from -6 to 6
- base_key_value: bfloat16 [8192, 8, 2, 128], P('narrow'), may hold values from -0.0625 to 0.0625
- store_a: bfloat16 [256, 8192, 128], P('wide', 'narrow'), may hold values from -0.0625 to 0.0625
- stored_up_maps: bfloat16 [256, 2, 64, 8, 128], P('wide', None, None, 'narrow'), may hold values from -0.75 to 0.75
- adapter_ids: int32 [512], P('wide'), may hold values from 0 to 255, as said below
- span_start: int32 [512], P('wide'), may hold values from 0 to 31
Outputs:
- key_value: bfloat16 [8, 65536, 2, 128], P('narrow', 'wide')
Inputs may be any that keep to these rules, and one draw needn't show every extreme that they name: `adapter_ids`: requests of one replica that name different adapters name adapters of different owners, the owner of adapter a being the replica a // 8.
All inputs are finite; a program needn't handle non-finite values.
Results may differ from a plain program's by a relative error of at most 0.015.
Values may be sent and summed in bfloat16 or wider, within the bound.
No kernel may reach another device: no remote copies, remote signals or barrier semaphores. Data moves between devices by JAX's collectives and lax.ppermute only.
A program may use at most 192 MiB of HBM per device.

v0:
```python
import jax
import jax.numpy as jnp
from jax import lax
from jax.sharding import PartitionSpec as P

THETA = 500000.0


def rotate_keys(values, positions):
    half_dim = values.shape[-1] // 2
    frequency = THETA ** (-(jnp.arange(half_dim, dtype=jnp.float32) * 2.0 / values.shape[-1]))
    angles = positions[:, None] * frequency[None, :]
    angles = jnp.concatenate([angles, angles], axis=-1)
    turned = jnp.concatenate([-values[..., half_dim:], values[..., :half_dim]], axis=-1)
    return values * jnp.cos(angles) + turned * jnp.sin(angles)


def shards(hidden, base_key_value, store_a, stored_up_maps, adapter_ids, span_start):
    wide_count = lax.axis_size("wide")
    stored = store_a.shape[0]
    requests = adapter_ids.shape[0]
    span_len = hidden.shape[0] // requests
    rank_two = store_a.shape[2]
    owners = adapter_ids // stored
    slot_ids = adapter_ids % stored
    matches = owners[None, :] == jnp.arange(wide_count, dtype=jnp.int32)[:, None]
    wanted = jnp.max(jnp.where(matches, slot_ids[None, :] + 1, 0), axis=1).reshape(wide_count, 1)
    asked_slots = lax.all_to_all(wanted, "wide", split_axis=0, concat_axis=0, tiled=True)
    filled = asked_slots[:, 0] > 0
    chosen = jnp.maximum(asked_slots[:, 0] - 1, 0)
    reply_a = jnp.where(filled[:, None, None], store_a[chosen], jnp.zeros((), jnp.bfloat16))
    reply_b = jnp.where(
        filled[:, None, None, None, None], stored_up_maps[chosen], jnp.zeros((), jnp.bfloat16)
    )
    got_a, got_b = (
        lax.all_to_all(reply_a, "wide", split_axis=0, concat_axis=0, tiled=True),
        lax.all_to_all(reply_b, "wide", split_axis=0, concat_axis=0, tiled=True),
    )
    needed_a = got_a[owners]
    needed_b = got_b[owners]
    request_rows = hidden.reshape(requests, span_len, hidden.shape[1])
    shrink_part = jnp.einsum(
        "rtd,rdc->rtc", request_rows, needed_a, preferred_element_type=jnp.float32
    )
    shrunk = lax.psum(shrink_part.astype(jnp.bfloat16), "narrow")
    base_total_sum = lax.psum_scatter(
        jnp.einsum(
            "td,dhjc->htjc", hidden, base_key_value, preferred_element_type=jnp.float32
        ).astype(jnp.bfloat16),
        "narrow",
        scatter_dimension=0,
        tiled=True,
    ).astype(jnp.float32)
    rank = rank_two // 2
    shrunk_split = shrunk.reshape(requests, span_len, 2, rank)
    delta = jnp.einsum(
        "rtjk,rjkhc->hrtjc", shrunk_split, needed_b, preferred_element_type=jnp.float32
    )
    raw = base_total_sum + delta.reshape(base_total_sum.shape)
    positions = (
        (span_start[:, None] * span_len + jnp.arange(span_len, dtype=jnp.int32)[None, :])
        .reshape(-1)
        .astype(jnp.float32)
    )
    keys_turned = jax.vmap(lambda head_keys: rotate_keys(head_keys, positions))(raw[:, :, 0, :])
    joined = jnp.stack([keys_turned, raw[:, :, 1, :]], axis=2)
    return joined.astype(jnp.bfloat16)


def solution(mesh):
    placed = (
        P("wide", "narrow"),
        P("narrow", None, None, None),
        P("wide", "narrow", None),
        P("wide", None, None, "narrow", None),
        P("wide"),
        P("wide"),
    )
    return jax.shard_map(
        shards,
        mesh=mesh,
        in_specs=placed,
        out_specs=P("narrow", "wide", None, None),
        check_vma=False,
    )
```

profile of v0, /device:TPU:1, one launch (start us, length us, event | category | flops | bytes accessed | tf_op | source)
XLA Modules:
  0.0 383.8 jit_solution(11532929862729622991)
XLA Ops:
  6.5 0.0 copy-start
  6.5 0.8 compare_select_fusion
  7.4 0.1 select_reduce_fusion
  7.4 0.1 copy.22
  7.5 20.4 %all_to_all.19 = s32[32,1,1]{2,1,0:T(1,128)S(1)} all-to-all(s32[32,1,1]{2,1,0:T(1,128)S(1)} %copy.22), channel_id=1, replica_groups=mesh['wide'=32,'narrow'=8] {'wide'}, dimensions={0} | all-to-all | bytes 256 | tf_op jit(solution)/shard_map/all_to_all | solution.py:28
  28.0 0.7 maximum_reduce_fusion
  28.6 0.0 copy-done
  28.6 4.8 %gather_fusion.2 = bf16[32,1024,128]{2,1,0:T(8,128)(2,1)} fusion(bf16[8,1024,128]{2,1,0:T(8,128)(2,1)S(1)} %copy-done, s32[1024]{0:T(1024)S(1)} %pad_clamp_fusion.1), kind=kCustom, calls=%fused_computation.2 | custom fusion | bytes 16777344 | tf_op jit(solution)/shard_map/gather | solution.py:31
  33.5 0.7 compare_reduce_fusion
  34.1 7.2 %broadcast_select_fusion = bf16[32,1024,128]{2,1,0:T(8,128)(2,1)} fusion(bf16[32,1024,128]{2,1,0:T(8,128)(2,1)} %gather_fusion.2, pred[32]{0:T(512)(128)(4,1)S(1)} %compare_reduce_fusion), kind=kLoop, calls=%fused_computation.5 | loop fusion | flops 4194304 | bytes 16777248 | tf_op jit(solution)/shard_map/jit(_where)/select_n | solution.py:31
  41.3 5.0 %all-to-all-start.2 = ((bf16[32,1024,128]{2,1,0:T(8,128)(2,1)}), bf16[32,1024,128]{2,1,0:T(8,128)(2,1)}, u32[]{:S(2)}, u32[]{:S(2)}) async-start(bf16[32,1024,128]{2,1,0:T(8,128)(2,1)} %broadcast_select_fusion), calls=%async_computation.3 | async-start | bytes 16777216 | tf_op jit(solution)/shard_map/all_to_all | solution.py:36
  46.3 0.0 all-reduce.2.cloned.1.call-start
  46.4 189.5 %all-to-all-done.2 = bf16[32,1024,128]{2,1,0:T(8,128)(2,1)} async-done(((bf16[32,1024,128]{2,1,0:T(8,128)(2,1)}), bf16[32,1024,128]{2,1,0:T(8,128)(2,1)}, u32[]{:S(2)}, u32[]{:S(2)}) %all-to-all-start.2) | async-done | bytes 8388640 | tf_op jit(solution)/shard_map/all_to_all | solution.py:36
  235.9 6.4 %gather_fusion.3 = bf16[16,1024,128]{2,1,0:T(8,128)(2,1)} fusion(bf16[32,1024,128]{2,1,0:T(8,128)(2,1)} %all-to-all-done.2, s32[1024]{0:T(1024)S(1)} %pad_clamp_fusion), kind=kCustom, calls=%fused_computation.3 | custom fusion | bytes 8388672 | tf_op jit(solution)/shard_map/gather | solution.py:39
  242.3 5.8 %convolution_convert_fusion = bf16[16,128,128]{2,1,0:T(8,128)(2,1)} fusion(bf16[16,1024,128]{2,1,0:T(8,128)(2,1)} %gather_fusion.3, bf16[16,128,1024]{2,1,0:T(8,128)(2,1)} %bitcast.39), kind=kOutput, calls=%fused_computation.10 | convolution fusion | flops 537133056 | bytes 8912896 | tf_op jit(solution)/shard_map/rtd,rdc->rtc/dot_general | solution.py:42
  248.1 0.0 all-reduce.2.cloned.1.call-update
  248.1 0.0 reduce-scatter.2.cloned.1.call-start
  248.2 14.5 %convert_bitcast_fusion = bf16[8,2048,2,128]{1,3,2,0:T(8,128)(2,1)} fusion(bf16[2048,1024]{1,0:T(8,128)(2,1)} %param.6, bf16[1024,8,2,128]{3,2,1,0:T(2,128)(2,1)} %param.7), kind=kOutput, calls=%fused_computation.4 | convolution fusion | flops 8594128896 | bytes 16777216 | tf_op jit(solution)/shard_map/td,dhjc->htjc/dot_general | solution.py:47
  262.6 0.0 copy-start.2
  262.6 0.0 reduce-scatter.2.cloned.1.call-update
  262.7 0.0 copy-start.3
  262.7 0.9 copy-done.2
  263.6 0.7 gather_fusion
  264.3 1.1 bitcast_select_fusion
  265.5 5.8 %all-to-all-start.1 = ((bf16[32,2,64,1,128]{4,2,1,3,0:T(8,128)(2,1)}), bf16[32,2,64,1,128]{4,2,1,3,0:T(8,128)(2,1)S(1)}, u32[]{:S(2)}, u32[]{:S(2)}) async-start(bf16[32,2,64,1,128]{4,2,1,3,0:T(8,128)(2,1)} %bitcast_select_fusion), calls=%async_computation.2 | async-start | bytes 2097152 | tf_op jit(solution)/shard_map/all_to_all | solution.py:37
  271.2 0.0 copy-done.3
  271.3 0.1 convert_bitcast_fusion.1
  271.3 0.1 multiply_bitcast_fusion
  271.4 25.2 %all-to-all-done.1 = bf16[32,2,64,1,128]{4,2,1,3,0:T(8,128)(2,1)S(1)} async-done(((bf16[32,2,64,1,128]{4,2,1,3,0:T(8,128)(2,1)}), bf16[32,2,64,1,128]{4,2,1,3,0:T(8,128)(2,1)S(1)}, u32[]{:S(2)}, u32[]{:S(2)}) %all-to-all-start.1) | async-done | bytes 1048608 | tf_op jit(solution)/shard_map/all_to_all | solution.py:37
  296.6 0.6 gather_fusion.1
  297.3 13.9 %all-reduce.2.cloned.1.call-done = bf16[16,128,2,64]{1,3,2,0:T(8,128)(2,1)} async-done(((bf16[16,128,2,64]{1,3,2,0:T(8,128)(2,1)}), bf16[16,128,2,64]{1,3,2,0:T(8,128)(2,1)}) %all-reduce.2.cloned.1.call-update) | async-done | bytes 524304 | tf_op jit(solution)/shard_map/psum | solution.py:45
  311.1 1.5 convolution_bitcast_fusion
  312.7 2.0 copy.24
  314.6 1.7 reshape.278
  316.4 52.8 %reduce-scatter.2.cloned.1.call-done = bf16[1,2048,2,128]{1,3,2,0:T(8,128)(2,1)} async-done(((bf16[8,2048,2,128]{1,3,2,0:T(8,128)(2,1)}), bf16[1,2048,2,128]{1,3,2,0:T(8,128)(2,1)}) %reduce-scatter.2.cloned.1.call-update) | async-done | bytes 1048592 | tf_op jit(solution)/shard_map/reduce_scatter | solution.py:46
  369.2 1.5 convert_add_fusion
  370.7 0.1 slice_bitcast_fusion
  370.7 0.1 slice.36
  370.8 0.0 copy-start.1
  370.8 0.1 fusion.8
  370.9 3.9 %fusion.6 = bf16[1,2048,1,128]{1,3,2,0:T(8,128)(2,1)S(1)} fusion(f32[1,2048,1,64]{1,3,2,0:T(8,128)S(1)} %multiply_bitcast_fusion, f32[1,2048,1,64]{1,3,2,0:T(8,128)S(1)} %get-tuple-element.8, f32[1,2048,1,64]{1,3,2,0:T(8,128)S(1)} %get-tuple-element.7, f32[1,2048,2,128]{1,3,2,0:T(8,128)S(1)} %convert_add_fusion), kind=kLoop, calls=%fused_computation.17 | loop fusion | flops 1572864 | bytes 3145728 | tf_op jit(solution)/shard_map/convert
  374.8 0.1 pad_maximum_fusion.1
  374.9 2.0 copy.25
  376.9 0.0 copy-done.1
  (4 shorter events, 0.0 us)
Async XLA Ops:
  6.5 22.1 %copy-start = (bf16[8,1024,128]{2,1,0:T(8,128)(2,1)S(1)}, bf16[8,1024,128]{2,1,0:T(8,128)(2,1)}, u32[]{:S(2)}) copy-start(bf16[8,1024,128]{2,1,0:T(8,128)(2,1)} %param.8) | copy-start | bytes 6291460
  41.3 194.5 %all-to-all-start.2 = ((bf16[32,1024,128]{2,1,0:T(8,128)(2,1)}), bf16[32,1024,128]{2,1,0:T(8,128)(2,1)}, u32[]{:S(2)}, u32[]{:S(2)}) async-start(bf16[32,1024,128]{2,1,0:T(8,128)(2,1)} %broadcast_select_fusion), calls=%async_computation.3 | async-start | bytes 16777216 | tf_op jit(solution)/shard_map/all_to_all | solution.py:36
  46.3 264.8 %all-reduce.2.cloned.1.call-start = ((), (), s32[]{:S(2)}) async-start(), calls=%async_computation.5 | async-start | bytes 1048576 | tf_op jit(solution)/shard_map/psum | solution.py:45
  248.1 121.1 %reduce-scatter.2.cloned.1.call-start = ((), (), s32[]{:S(2)}) async-start(), calls=%async_computation.4 | async-start | bytes 9437184 | tf_op jit(solution)/shard_map/reduce_scatter | solution.py:46
  262.6 1.0 copy-start.2
  262.7 8.6 %copy-start.3 = (s32[16]{0:T(128)S(1)}, s32[16]{0:T(128)}, u32[]{:S(2)}) copy-start(s32[16]{0:T(128)} %param.11) | copy-start | bytes 196
  265.5 31.1 %all-to-all-start.1 = ((bf16[32,2,64,1,128]{4,2,1,3,0:T(8,128)(2,1)}), bf16[32,2,64,1,128]{4,2,1,3,0:T(8,128)(2,1)S(1)}, u32[]{:S(2)}, u32[]{:S(2)}) async-start(bf16[32,2,64,1,128]{4,2,1,3,0:T(8,128)(2,1)} %bitcast_select_fusion), calls=%async_computation.2 | async-start | bytes 2097152 | tf_op jit(solution)/shard_map/all_to_all | solution.py:37
  370.8 6.1 %copy-start.1 = (bf16[8,1024,128]{2,1,0:T(8,128)(2,1)S(1)}, bf16[8,1024,128]{2,1,0:T(8,128)(2,1)}, u32[]{:S(2)}) copy-start(bf16[8,1024,128]{2,1,0:T(8,128)(2,1)} %param.8) | copy-start | bytes 6291460
Sparse Core Ops, SparseCore 0:
  248.2 62.8 all-reduce.1
  313.7 55.4 reduce-scatter.1
where the time goes:
time: 384 us
  waiting for transfers between devices  281 us (73%)
  matrix products  21.8 us (6%)
  blocking collectives  20.4 us (5%)
  local copies, waits for them, and re-layouts  19.5 us (5%)
  other arithmetic  16.3 us (4%)
  between operations  13.6 us (4%)
  starting transfers between devices  10.8 us (3%)
    all_to_all x1, waiting for transfers between devices, shards(): lax.all_to_all(reply_a, 'wide', split_axis=0, concat_axis=0, tiled=True)  190 us
    reduce_scatter x1, waiting for transfers between devices, shards(): lax.psum_scatter(jnp.einsum('td,dhjc->htjc', hidden, base_key_value, pref...  52.8 us
    all_to_all x1, waiting for transfers between devices, shards(): lax.all_to_all(reply_b, 'wide', split_axis=0, concat_axis=0, tiled=True)  25.2 us
    all_to_all x1, blocking collectives, shards(): lax.all_to_all(wanted, 'wide', split_axis=0, concat_axis=0, tiled=True)  20.4 us
    dot_general x1, matrix products, shards(): jnp.einsum('td,dhjc->htjc', hidden, base_key_value, preferred_element_typ...  14.5 us
    psum x1, waiting for transfers between devices, shards(): shrunk = lax.psum(shrink_part.astype(jnp.bfloat16), 'narrow')  13.9 us
  transfers between devices with their start and end apart: 4, of which 4 were waited for; matrix products, arithmetic and copies ran while one was open for 6% of the time, Pallas kernels for 0%

commit v1 on v0

v1 whole, which is shorter than its diff:
```python
import jax
import jax.numpy as jnp
from jax import lax
from jax.sharding import PartitionSpec as P


THETA = 500000.0


def rotate_keys(values, positions):
    half_dim = values.shape[-1] // 2
    frequency = THETA ** (-(jnp.arange(half_dim, dtype=jnp.float32) * 2.0 / values.shape[-1]))
    angles = positions[:, None] * frequency[None, :]
    angles = jnp.concatenate([angles, angles], axis=-1)
    turned = jnp.concatenate([-values[..., half_dim:], values[..., :half_dim]], axis=-1)
    return values * jnp.cos(angles) + turned * jnp.sin(angles)


def shards(hidden, base_key_value, store_a, stored_up_maps, adapter_ids, span_start):
    wide_count = lax.axis_size("wide")
    me = lax.axis_index("wide")
    stored = store_a.shape[0]
    requests = adapter_ids.shape[0]
    span_len = hidden.shape[0] // requests
    width = store_a.shape[1]
    rank_two = store_a.shape[2]
    rank = rank_two // 2
    heads_here = stored_up_maps.shape[3]
    head_size = stored_up_maps.shape[4]

    all_ids = lax.all_gather(adapter_ids, "wide", tiled=True).reshape(wide_count, requests)
    asked = all_ids // stored == me
    chosen = jnp.max(jnp.where(asked, all_ids % stored, 0), axis=1)

    up_rows = stored_up_maps.reshape(stored, 2 * rank * heads_here, head_size)
    packed = jnp.concatenate([store_a, up_rows], axis=1)
    reply = packed[chosen]
    got = lax.all_to_all(reply, "wide", split_axis=0, concat_axis=0, tiled=True)

    partials = jnp.einsum(
        "td,dhjc->htjc", hidden, base_key_value, preferred_element_type=jnp.float32
    ).astype(jnp.bfloat16)
    base_total_sum = lax.psum_scatter(
        partials, "narrow", scatter_dimension=0, tiled=True
    )
    got, base_total_sum = lax.optimization_barrier((got, base_total_sum))
    base_total_sum = base_total_sum.astype(jnp.float32)

    owners = adapter_ids // stored
    needed = got[owners]
    needed_a = needed[:, :width]
    needed_b = needed[:, width:].reshape(requests, 2, rank, heads_here, head_size)
    request_rows = hidden.reshape(requests, span_len, hidden.shape[1])
    shrink_part = jnp.einsum(
        "rtd,rdc->rtc", request_rows, needed_a, preferred_element_type=jnp.float32
    )
    shrunk = lax.psum(shrink_part.astype(jnp.bfloat16), "narrow")
    shrunk_split = shrunk.reshape(requests, span_len, 2, rank)
    delta = jnp.einsum(
        "rtjk,rjkhc->hrtjc", shrunk_split, needed_b, preferred_element_type=jnp.float32
    )
    raw = base_total_sum + delta.reshape(base_total_sum.shape)
    positions = (
        (span_start[:, None] * span_len + jnp.arange(span_len, dtype=jnp.int32)[None, :])
        .reshape(-1)
        .astype(jnp.float32)
    )
    keys_turned = jax.vmap(lambda head_keys: rotate_keys(head_keys, positions))(raw[:, :, 0, :])
    joined = jnp.stack([keys_turned, raw[:, :, 1, :]], axis=2)
    return joined.astype(jnp.bfloat16)


def solution(mesh):
    placed = (
        P("wide", "narrow"),
        P("narrow", None, None, None),
        P("wide", "narrow", None),
        P("wide", None, None, "narrow", None),
        P("wide"),
        P("wide"),
    )
    return jax.shard_map(
        shards,
        mesh=mesh,
        in_specs=placed,
        out_specs=P("narrow", "wide", None, None),
        check_vma=False,
    )
```

time: 384 us -> 346 us (0.901)
  waiting for transfers between devices: 281 us -> 255 us
  other arithmetic: 16.3 us -> 7.76 us
  starting transfers between devices: 10.8 us -> 5.05 us
    all_to_all x2 -> x1, waiting for transfers between devices: 215 us -> 126 us  [shards(): got = lax.all_to_all(reply, 'wide', split_axis=0, concat_axis=0, tiled=True)]
    psum x1, waiting for transfers between devices: 13.9 us -> 69.1 us  [shards(): shrunk = lax.psum(shrink_part.astype(jnp.bfloat16), 'narrow')]
    all_to_all x1 -> x0, blocking collectives: 20.4 us -> none  [shards(): lax.all_to_all(wanted, 'wide', split_axis=0, concat_axis=0, tiled=True)]
    unnamed x0 -> x1, blocking collectives: none -> 20 us
    select_n x3 -> x2, other arithmetic: 9.15 us -> 0.02 us  [the longest x1 0.01 us: shards(): needed = got[owners]]
    reduce_scatter x1, waiting for transfers between devices: 52.8 us -> 59.4 us  [shards(): lax.psum_scatter(partials, 'narrow', scatter_dimension=0, tiled=True)]
    all_to_all x2 -> x1, starting transfers between devices: 10.7 us -> 4.97 us  [shards(): got = lax.all_to_all(reply, 'wide', split_axis=0, concat_axis=0, tiled=True)]
    gather x4 -> x2, local copies, waits for them, and re-layouts: 12.6 us -> 12.5 us  [the longest x1 7.07 us: shards(): needed = got[owners]]
  transfers between devices with their start and end apart: 4 -> 3, of which waited for: 4 -> 3; matrix products, arithmetic and copies ran while one was open for 6% -> 4% of each run, Pallas kernels for 0% -> 0%
where the time goes in v1:
time: 346 us; the launch traced here: 345 us
  waiting for transfers between devices  255 us (74%)
  matrix products  21.8 us (6%)
  local copies, waits for them, and re-layouts  21.1 us (6%)
  blocking collectives  20 us (6%)
  between operations  14.2 us (4%)
  other arithmetic  7.76 us (2%)
  starting transfers between devices  5.05 us (1%)
    all_to_all x1, waiting for transfers between devices, shards(): got = lax.all_to_all(reply, 'wide', split_axis=0, concat_axis=0, tiled=True)  126 us
    psum x1, waiting for transfers between devices, shards(): shrunk = lax.psum(shrink_part.astype(jnp.bfloat16), 'narrow')  69.1 us
    reduce_scatter x1, waiting for transfers between devices, shards(): lax.psum_scatter(partials, 'narrow', scatter_dimension=0, tiled=True)  59.4 us
    unnamed x1, blocking collectives  20 us
    dot_general x1, matrix products, shards(): jnp.einsum('td,dhjc->htjc', hidden, base_key_value, preferred_element_typ...  14.5 us
    gather x1, local copies, waits for them, and re-layouts, shards(): needed = got[owners]  7.07 us
  transfers between devices with their start and end apart: 3, of which 3 were waited for; matrix products, arithmetic and copies ran while one was open for 4% of the time, Pallas kernels for 0%

profile of v1, /device:TPU:1, one launch (start us, length us, event | category | flops | bytes accessed | tf_op | source)
XLA Modules:
  0.0 344.6 jit_solution(7920450730013967619)
XLA Ops:
  6.5 1.3 dynamic-slice
  8.5 0.9 dynamic-update-slice
  9.3 20.0 %all-reduce = s32[512]{0:T(512)S(1)} all-reduce(s32[512]{0:T(512)S(1)} %dynamic-update-slice), channel_id=1, replica_groups=mesh['wide'=32,'narrow'=8] {'wide'}, use_global_device_ids=true, to_apply=%add | all-reduce | flops 512 | bytes 4096
  29.3 0.1 reshape.254
  29.4 0.1 fusion.16
  29.6 1.9 pad_maximum_fusion
  31.4 5.4 %gather_fusion = bf16[32,1152,128]{2,1,0:T(8,128)(2,1)} fusion(bf16[8,1152,128]{2,1,0:T(8,128)(2,1)S(1)} %pad_maximum_fusion, s32[1024]{0:T(1024)S(1)} %pad_clamp_fusion.1), kind=kCustom, calls=%fused_computation | custom fusion | bytes 18874496 | tf_op jit(solution)/shard_map/gather | solution.py:37
  36.8 5.0 %all-to-all-start = ((bf16[32,1152,128]{2,1,0:T(8,128)(2,1)}), bf16[32,1152,128]{2,1,0:T(8,128)(2,1)}, u32[]{:S(2)}, u32[]{:S(2)}) async-start(bf16[32,1152,128]{2,1,0:T(8,128)(2,1)} %gather_fusion), calls=%async_computation | async-start | bytes 18874368 | tf_op jit(solution)/shard_map/all_to_all | solution.py:38
  41.8 0.0 reduce-scatter.2.cloned.1.call-start
  41.8 14.5 %convert_bitcast_fusion = bf16[8,2048,2,128]{1,3,2,0:T(8,128)(2,1)} fusion(bf16[2048,1024]{1,0:T(8,128)(2,1)} %param.6, bf16[1024,8,2,128]{3,2,1,0:T(2,128)(2,1)} %param.7), kind=kOutput, calls=%fused_computation.2 | convolution fusion | flops 8594128896 | bytes 16777216 | tf_op jit(solution)/shard_map/td,dhjc->htjc/dot_general | solution.py:40
  56.4 0.0 copy-start
  56.4 0.0 copy-start.1
  56.4 0.0 reduce-scatter.2.cloned.1.call-update
  56.4 0.0 all-reduce.3.cloned.1.call-start
  56.5 0.6 copy-done
  57.1 0.0 copy-done.1
  57.1 0.1 convert_bitcast_fusion.1
  57.2 59.4 %reduce-scatter.2.cloned.1.call-done = bf16[1,2048,2,128]{1,3,2,0:T(8,128)(2,1)} async-done(((bf16[8,2048,2,128]{1,3,2,0:T(8,128)(2,1)}), bf16[1,2048,2,128]{1,3,2,0:T(8,128)(2,1)}) %reduce-scatter.2.cloned.1.call-update) | async-done | bytes 1048592 | tf_op jit(solution)/shard_map/reduce_scatter | solution.py:43
  116.6 126.2 %all-to-all-done = bf16[32,1152,128]{2,1,0:T(8,128)(2,1)} async-done(((bf16[32,1152,128]{2,1,0:T(8,128)(2,1)}), bf16[32,1152,128]{2,1,0:T(8,128)(2,1)}, u32[]{:S(2)}, u32[]{:S(2)}) %all-to-all-start) | async-done | bytes 9437216 | tf_op jit(solution)/shard_map/all_to_all | solution.py:38
  242.7 7.1 %gather_fusion.1 = bf16[16,1152,128]{2,1,0:T(8,128)(2,1)} fusion(bf16[32,1152,128]{2,1,0:T(8,128)(2,1)} %all-to-all-done, s32[1024]{0:T(1024)S(1)} %pad_clamp_fusion), kind=kCustom, calls=%fused_computation.1 | custom fusion | bytes 9437248 | tf_op jit(solution)/shard_map/gather | solution.py:50
  249.8 0.0 slice-start
  249.8 5.8 %fusion.4 = bf16[16,128,128]{2,1,0:T(8,128)(2,1)} fusion(bf16[16,128,1024]{2,1,0:T(8,128)(2,1)} %bitcast.42, bf16[16,1152,128]{2,1,0:T(8,128)(2,1)} %gather_fusion.1), kind=kOutput, calls=%fused_computation.10 | convolution fusion | flops 537133056 | bytes 8912896 | tf_op jit(solution)/shard_map/rtd,rdc->rtc/dot_general | solution.py:54
  255.6 0.0 all-reduce.3.cloned.1.call-update
  255.6 0.1 multiply_bitcast_fusion
  255.7 69.1 %all-reduce.3.cloned.1.call-done = bf16[16,128,2,64]{1,3,2,0:T(8,128)(2,1)} async-done(((bf16[16,128,2,64]{1,3,2,0:T(8,128)(2,1)}), bf16[16,128,2,64]{1,3,2,0:T(8,128)(2,1)}) %all-reduce.3.cloned.1.call-update) | async-done | bytes 524304 | tf_op jit(solution)/shard_map/psum | solution.py:57
  324.8 0.0 slice-done
  324.8 1.5 convolution_bitcast_fusion
  326.3 2.0 copy.13
  328.4 1.7 reshape.258
  330.1 1.5 convert_add_fusion
  331.6 0.1 slice_bitcast_fusion
  331.7 0.1 slice.46
  331.7 0.1 fusion.13
  331.8 3.9 %fusion.11 = bf16[1,2048,1,128]{1,3,2,0:T(8,128)(2,1)S(1)} fusion(f32[1,2048,1,64]{1,3,2,0:T(8,128)S(1)} %multiply_bitcast_fusion, f32[1,2048,1,64]{1,3,2,0:T(8,128)S(1)} %get-tuple-element.10, f32[1,2048,1,64]{1,3,2,0:T(8,128)S(1)} %get-tuple-element.9, f32[1,2048,2,128]{1,3,2,0:T(8,128)S(1)} %convert_add_fusion), kind=kLoop, calls=%fused_computation.17 | loop fusion | flops 1572864 | bytes 3145728 | tf_op jit(solution)/shard_map/convert
  335.7 0.1 pad_maximum_fusion.2
  335.8 2.0 copy.14
  (7 shorter events, 0.0 us)
Async XLA Ops:
  36.8 205.9 %all-to-all-start = ((bf16[32,1152,128]{2,1,0:T(8,128)(2,1)}), bf16[32,1152,128]{2,1,0:T(8,128)(2,1)}, u32[]{:S(2)}, u32[]{:S(2)}) async-start(bf16[32,1152,128]{2,1,0:T(8,128)(2,1)} %gather_fusion), calls=%async_computation | async-start | bytes 18874368 | tf_op jit(solution)/shard_map/all_to_all | solution.py:38
  41.8 74.8 %reduce-scatter.2.cloned.1.call-start = ((), (), s32[]{:S(2)}) async-start(), calls=%async_computation.2 | async-start | bytes 9437184 | tf_op jit(solution)/shard_map/reduce_scatter | solution.py:43
  56.4 0.7 copy-start
  56.4 0.7 copy-start.1
  56.4 268.4 %all-reduce.3.cloned.1.call-start = ((), (), s32[]{:S(2)}) async-start(), calls=%async_computation.3 | async-start | bytes 1048576 | tf_op jit(solution)/shard_map/psum | solution.py:57
  249.8 75.0 %slice-start = ((bf16[16,1152,128]{2,1,0:T(8,128)(2,1)}), bf16[16,128,128]{2,1,0:T(8,128)(2,1)S(1)}, s32[]{:S(2)}) async-start(bf16[16,1152,128]{2,1,0:T(8,128)(2,1)} %gather_fusion.1), calls=%async_computation.4 | async-start | bytes 1048576 | tf_op jit(solution)/shard_map/slice | solution.py:52
Sparse Core Ops, SparseCore 0:
  56.5 59.9 reduce-scatter.1
  255.7 69.0 all-reduce.2

commit v2 on v1

--- a/solution.py
+++ b/solution.py
@@ -18,7 +18,6 @@
 
 def shards(hidden, base_key_value, store_a, stored_up_maps, adapter_ids, span_start):
     wide_count = lax.axis_size("wide")
-    me = lax.axis_index("wide")
     stored = store_a.shape[0]
     requests = adapter_ids.shape[0]
     span_len = hidden.shape[0] // requests
@@ -28,9 +27,12 @@
     heads_here = stored_up_maps.shape[3]
     head_size = stored_up_maps.shape[4]
 
-    all_ids = lax.all_gather(adapter_ids, "wide", tiled=True).reshape(wide_count, requests)
-    asked = all_ids // stored == me
-    chosen = jnp.max(jnp.where(asked, all_ids % stored, 0), axis=1)
+    owners = adapter_ids // stored
+    matches = owners[None, :] == jnp.arange(wide_count, dtype=jnp.int32)[:, None]
+    wanted = jnp.max(jnp.where(matches, adapter_ids % stored, 0), axis=1)
+    chosen = lax.all_to_all(
+        wanted.reshape(wide_count, 1), "wide", split_axis=0, concat_axis=0, tiled=True
+    )[:, 0]
 
     up_rows = stored_up_maps.reshape(stored, 2 * rank * heads_here, head_size)
     packed = jnp.concatenate([store_a, up_rows], axis=1)
@@ -46,7 +48,6 @@
     got, base_total_sum = lax.optimization_barrier((got, base_total_sum))
     base_total_sum = base_total_sum.astype(jnp.float32)
 
-    owners = adapter_ids // stored
     needed = got[owners]
     needed_a = needed[:, :width]
     needed_b = needed[:, width:].reshape(requests, 2, rank, heads_here, head_size)
@@ -54,7 +55,7 @@
     shrink_part = jnp.einsum(
         "rtd,rdc->rtc", request_rows, needed_a, preferred_element_type=jnp.float32
     )
-    shrunk = lax.psum(shrink_part.astype(jnp.bfloat16), "narrow")
+    shrunk = lax.psum(shrink_part, "narrow").astype(jnp.bfloat16)
     shrunk_split = shrunk.reshape(requests, span_len, 2, rank)
     delta = jnp.einsum(
         "rtjk,rjkhc->hrtjc", shrunk_split, needed_b, preferred_element_type=jnp.float32

time: 346 us -> 338 us (0.977)
  waiting for transfers between devices: 255 us -> 206 us
  blocking collectives: 20 us -> 50.6 us
  starting transfers between devices: 5.05 us -> 17 us
    psum x1 -> x0, waiting for transfers between devices: 69.1 us -> none  [shards(): shrunk = lax.psum(shrink_part.astype(jnp.bfloat16), 'narrow')]
    psum x0 -> x1, blocking collectives: none -> 50.6 us  [shards(): shrunk = lax.psum(shrink_part, 'narrow').astype(jnp.bfloat16)]
    unnamed x1 -> x0, blocking collectives: 20 us -> none
    all_to_all x1, waiting for transfers between devices: 126 us -> 144 us  [shards(): got = lax.all_to_all(reply, 'wide', split_axis=0, concat_axis=0, tiled=True)]
    all_to_all x0 -> x1, starting transfers between devices: none -> 12 us  [shards(): lax.all_to_all(wanted.reshape(wide_count, 1), 'wide', split_axis=0, conca...]
    all_to_all x0 -> x1, waiting for transfers between devices: none -> 6.67 us  [shards(): lax.all_to_all(wanted.reshape(wide_count, 1), 'wide', split_axis=0, conca...]
    reduce_scatter x1, waiting for transfers between devices: 59.4 us -> 55.6 us  [shards(): lax.psum_scatter(partials, 'narrow', scatter_dimension=0, tiled=True)]
  transfers between devices with their start and end apart: 3 -> 3, of which waited for: 3 -> 3; matrix products, arithmetic and copies ran while one was open for 4% -> 5% of each run, Pallas kernels for 0% -> 0%
where the time goes in v2:
time: 338 us; the launch traced here: 336 us
  waiting for transfers between devices  206 us (61%)
  blocking collectives  50.6 us (15%)
  local copies, waits for them, and re-layouts  20.2 us (6%)
  matrix products  19.8 us (6%)
  starting transfers between devices  17 us (5%)
  between operations  13.6 us (4%)
  other arithmetic  8.57 us (3%)
    all_to_all x1, waiting for transfers between devices, shards(): got = lax.all_to_all(reply, 'wide', split_axis=0, concat_axis=0, tiled=True)  144 us
    reduce_scatter x1, waiting for transfers between devices, shards(): lax.psum_scatter(partials, 'narrow', scatter_dimension=0, tiled=True)  55.6 us
    psum x1, blocking collectives, shards(): shrunk = lax.psum(shrink_part, 'narrow').astype(jnp.bfloat16)  50.6 us
    dot_general x1, matrix products, shards(): jnp.einsum('td,dhjc->htjc', hidden, base_key_value, preferred_element_typ...  14.4 us
    all_to_all x1, starting transfers between devices, shards(): lax.all_to_all(wanted.reshape(wide_count, 1), 'wide', split_axis=0, conca...  12 us
    gather x1, local copies, waits for them, and re-layouts, shards(): needed = got[owners]  7.07 us
  transfers between devices with their start and end apart: 3, of which 3 were waited for; matrix products, arithmetic and copies ran while one was open for 5% of the time, Pallas kernels for 0%

profile of v2, /device:TPU:1, one launch (start us, length us, event | category | flops | bytes accessed | tf_op | source)
XLA Modules:
  0.0 336.0 jit_solution(17585997684332703841)
XLA Ops:
  6.5 0.7 compare_select_fusion
  7.2 0.1 select_reduce_fusion
  7.3 0.7 copy.25
  8.0 12.0 %all-to-all-start = ((s32[32,1,1]{2,1,0:T(1,128)}), s32[32,1,1]{2,1,0:T(1,128)S(1)}, u32[]{:S(2)}, u32[]{:S(2)}) async-start(s32[32,1,1]{2,1,0:T(1,128)} %copy.25), calls=%async_computation | async-start | bytes 32768 | tf_op jit(solution)/shard_map/all_to_all | solution.py:33
  20.0 1.9 pad_maximum_fusion
  21.9 6.7 %all-to-all-done = s32[32,1,1]{2,1,0:T(1,128)S(1)} async-done(((s32[32,1,1]{2,1,0:T(1,128)}), s32[32,1,1]{2,1,0:T(1,128)S(1)}, u32[]{:S(2)}, u32[]{:S(2)}) %all-to-all-start) | async-done | bytes 160 | tf_op jit(solution)/shard_map/all_to_all | solution.py:33
  28.6 0.7 reduce
  29.2 5.4 %gather_fusion = bf16[32,1152,128]{2,1,0:T(8,128)(2,1)} fusion(bf16[8,1152,128]{2,1,0:T(8,128)(2,1)S(1)} %pad_maximum_fusion, s32[1024]{0:T(1024)S(1)} %pad_clamp_fusion.1), kind=kCustom, calls=%fused_computation | custom fusion | bytes 18874496 | tf_op jit(solution)/shard_map/gather | solution.py:39
  34.6 5.0 %all-to-all-start.1 = ((bf16[32,1152,128]{2,1,0:T(8,128)(2,1)}), bf16[32,1152,128]{2,1,0:T(8,128)(2,1)}, u32[]{:S(2)}, u32[]{:S(2)}) async-start(bf16[32,1152,128]{2,1,0:T(8,128)(2,1)} %gather_fusion), calls=%async_computation.1 | async-start | bytes 18874368 | tf_op jit(solution)/shard_map/all_to_all | solution.py:40
  39.6 0.0 reduce-scatter.2.cloned.1.call-start
  39.7 14.4 %convert_bitcast_fusion = bf16[8,2048,2,128]{1,3,2,0:T(8,128)(2,1)} fusion(bf16[2048,1024]{1,0:T(8,128)(2,1)} %param.6, bf16[1024,8,2,128]{3,2,1,0:T(2,128)(2,1)} %param.7), kind=kOutput, calls=%fused_computation.2 | convolution fusion | flops 8594128896 | bytes 16777216 | tf_op jit(solution)/shard_map/td,dhjc->htjc/dot_general | solution.py:42
  54.1 0.0 copy-start.2
  54.1 0.0 reduce-scatter.2.cloned.1.call-update
  54.1 0.6 copy-done.2
  54.7 0.1 convert_bitcast_fusion.1
  54.8 0.9 multiply_bitcast_fusion
  55.7 55.6 %reduce-scatter.2.cloned.1.call-done = bf16[1,2048,2,128]{1,3,2,0:T(8,128)(2,1)} async-done(((bf16[8,2048,2,128]{1,3,2,0:T(8,128)(2,1)}), bf16[1,2048,2,128]{1,3,2,0:T(8,128)(2,1)}) %reduce-scatter.2.cloned.1.call-update) | async-done | bytes 1048592 | tf_op jit(solution)/shard_map/reduce_scatter | solution.py:45
  111.3 144.0 %all-to-all-done.1 = bf16[32,1152,128]{2,1,0:T(8,128)(2,1)} async-done(((bf16[32,1152,128]{2,1,0:T(8,128)(2,1)}), bf16[32,1152,128]{2,1,0:T(8,128)(2,1)}, u32[]{:S(2)}, u32[]{:S(2)}) %all-to-all-start.1) | async-done | bytes 9437216 | tf_op jit(solution)/shard_map/all_to_all | solution.py:40
  255.3 7.1 %gather_fusion.1 = bf16[16,1152,128]{2,1,0:T(8,128)(2,1)} fusion(bf16[32,1152,128]{2,1,0:T(8,128)(2,1)} %all-to-all-done.1, s32[1024]{0:T(1024)S(1)} %pad_clamp_fusion), kind=kCustom, calls=%fused_computation.1 | custom fusion | bytes 9437248 | tf_op jit(solution)/shard_map/gather | solution.py:51
  262.4 0.0 slice-start
  262.4 4.8 %fusion.4 = f32[16,128,128]{1,2,0:T(8,128)S(1)} fusion(bf16[16,128,1024]{2,1,0:T(8,128)(2,1)} %bitcast.43, bf16[16,1152,128]{2,1,0:T(8,128)(2,1)} %gather_fusion.1), kind=kOutput, calls=%fused_computation.10 | convolution fusion | flops 536870912 | bytes 9437184 | tf_op jit(solution)/shard_map/rtd,rdc->rtc/dot_general | solution.py:55
  267.2 50.6 %all-reduce.1 = bf16[16,128,128]{1,2,0:T(8,128)(2,1)S(1)} all-reduce(f32[16,128,128]{1,2,0:T(8,128)S(1)} %fusion.4), channel_id=1, replica_groups=mesh['wide'=32,'narrow'=8] {'narrow'}, use_global_device_ids=true, to_apply=%region_2.3 | all-reduce | flops 262144 | bytes 1572864 | tf_op jit(solution)/shard_map/psum | solution.py:58
  317.9 0.0 slice-done
  317.9 0.5 convolution_bitcast_fusion
  318.4 0.0 copy-start.1
  318.4 2.0 copy.28
  320.4 1.7 reshape.273
  322.1 0.0 copy-done.1
  322.1 0.0 copy-start
  322.1 0.3 convert_add_fusion
  322.4 0.1 slice_bitcast_fusion
  322.5 0.1 slice.46
  322.6 0.1 fusion.13
  322.7 0.5 copy-done
  323.2 3.9 %fusion.11 = bf16[1,2048,1,128]{1,3,2,0:T(8,128)(2,1)S(1)} fusion(f32[1,2048,1,64]{1,3,2,0:T(8,128)S(1)} %copy-done, f32[1,2048,1,64]{1,3,2,0:T(8,128)S(1)} %get-tuple-element.12, f32[1,2048,1,64]{1,3,2,0:T(8,128)S(1)} %get-tuple-element.11, f32[1,2048,2,128]{1,3,2,0:T(8,128)S(1)} %convert_add_fusion), kind=kLoop, calls=%fused_computation.17 | loop fusion | flops 1572864 | bytes 3145728 | tf_op jit(solution)/shard_map/convert
  327.0 0.1 pad_maximum_fusion.2
  327.1 2.0 copy.29
  (5 shorter events, 0.0 us)
Async XLA Ops:
  8.0 20.6 %all-to-all-start = ((s32[32,1,1]{2,1,0:T(1,128)}), s32[32,1,1]{2,1,0:T(1,128)S(1)}, u32[]{:S(2)}, u32[]{:S(2)}) async-start(s32[32,1,1]{2,1,0:T(1,128)} %copy.25), calls=%async_computation | async-start | bytes 32768 | tf_op jit(solution)/shard_map/all_to_all | solution.py:33
  34.6 220.7 %all-to-all-start.1 = ((bf16[32,1152,128]{2,1,0:T(8,128)(2,1)}), bf16[32,1152,128]{2,1,0:T(8,128)(2,1)}, u32[]{:S(2)}, u32[]{:S(2)}) async-start(bf16[32,1152,128]{2,1,0:T(8,128)(2,1)} %gather_fusion), calls=%async_computation.1 | async-start | bytes 18874368 | tf_op jit(solution)/shard_map/all_to_all | solution.py:40
  39.6 71.7 %reduce-scatter.2.cloned.1.call-start = ((), (), s32[]{:S(2)}) async-start(), calls=%async_computation.3 | async-start | bytes 9437184 | tf_op jit(solution)/shard_map/reduce_scatter | solution.py:45
  54.1 0.7 copy-start.2
  262.4 55.5 %slice-start = ((bf16[16,1152,128]{2,1,0:T(8,128)(2,1)}), bf16[16,128,128]{2,1,0:T(8,128)(2,1)S(1)}, s32[]{:S(2)}) async-start(bf16[16,1152,128]{2,1,0:T(8,128)(2,1)} %gather_fusion.1), calls=%async_computation.4 | async-start | bytes 1048576 | tf_op jit(solution)/shard_map/slice | solution.py:53
  318.4 3.8 %copy-start.1 = (bf16[1,2048,2,128]{1,3,2,0:T(8,128)(2,1)S(1)}, bf16[1,2048,2,128]{1,3,2,0:T(8,128)(2,1)}, u32[]{:S(2)}) copy-start(bf16[1,2048,2,128]{1,3,2,0:T(8,128)(2,1)} %reduce-scatter.2.cloned.1.call-done) | copy-start | bytes 3145732
  322.1 1.0 copy-start
Sparse Core Ops, SparseCore 0:
  54.2 57.0 reduce-scatter.1

commit v3 on v2

--- a/solution.py
+++ b/solution.py
@@ -14,6 +14,33 @@
     angles = jnp.concatenate([angles, angles], axis=-1)
     turned = jnp.concatenate([-values[..., half_dim:], values[..., :half_dim]], axis=-1)
     return values * jnp.cos(angles) + turned * jnp.sin(angles)
+
+
+def narrow_sum(v):
+    count = lax.axis_size("narrow")
+    me = lax.axis_index("narrow")
+    bits = []
+    bit = 1
+    while bit < count:
+        bits.append(bit)
+        bit *= 2
+    cur = v
+    for bit in bits:
+        half = cur.shape[0] // 2
+        upper = (me & bit) > 0
+        send = jnp.where(upper, cur[:half], cur[half:])
+        keep = jnp.where(upper, cur[half:], cur[:half])
+        pairs = [(i, i ^ bit) for i in range(count)]
+        cur = keep + lax.ppermute(send, "narrow", pairs)
+    cur = cur.astype(jnp.bfloat16)
+    for bit in reversed(bits):
+        upper = (me & bit) > 0
+        pairs = [(i, i ^ bit) for i in range(count)]
+        other = lax.ppermute(cur, "narrow", pairs)
+        cur = jnp.where(
+            upper, jnp.concatenate([other, cur]), jnp.concatenate([cur, other])
+        )
+    return cur
 
 
 def shards(hidden, base_key_value, store_a, stored_up_maps, adapter_ids, span_start):
@@ -55,7 +82,7 @@
     shrink_part = jnp.einsum(
         "rtd,rdc->rtc", request_rows, needed_a, preferred_element_type=jnp.float32
     )
-    shrunk = lax.psum(shrink_part, "narrow").astype(jnp.bfloat16)
+    shrunk = narrow_sum(shrink_part.reshape(requests * span_len, rank_two))
     shrunk_split = shrunk.reshape(requests, span_len, 2, rank)
     delta = jnp.einsum(
         "rtjk,rjkhc->hrtjc", shrunk_split, needed_b, preferred_element_type=jnp.float32

time: 338 us -> 318 us (0.941)
  blocking collectives: 50.6 us -> 0 us
  waiting for transfers between devices: 206 us -> 224 us
  starting transfers between devices: 17 us -> 31.4 us
    psum x1 -> x0, blocking collectives: 50.6 us -> none  [shards(): shrunk = lax.psum(shrink_part, 'narrow').astype(jnp.bfloat16)]
    ppermute x0 -> x6, waiting for transfers between devices: none -> 16 us  [the longest x3 10.2 us: narrow_sum(): cur = keep + lax.ppermute(send, 'narrow', pairs)]
    ppermute x0 -> x6, starting transfers between devices: none -> 14.3 us  [the longest x3 8.68 us: narrow_sum(): other = lax.ppermute(cur, 'narrow', pairs)]
  transfers between devices with their start and end apart: 3 -> 9, of which waited for: 3 -> 9; matrix products, arithmetic and copies ran while one was open for 5% -> 5% of each run, Pallas kernels for 0% -> 0%
where the time goes in v3:
time: 318 us
  waiting for transfers between devices  224 us (70%)
  starting transfers between devices  31.4 us (10%)
  matrix products  19.6 us (6%)
  local copies, waits for them, and re-layouts  19.5 us (6%)
  between operations  13.6 us (4%)
  other arithmetic  9.55 us (3%)
    all_to_all x1, waiting for transfers between devices, shards(): got = lax.all_to_all(reply, 'wide', split_axis=0, concat_axis=0, tiled=True)  144 us
    reduce_scatter x1, waiting for transfers between devices, shards(): lax.psum_scatter(partials, 'narrow', scatter_dimension=0, tiled=True)  57.2 us
    dot_general x1, matrix products, shards(): jnp.einsum('td,dhjc->htjc', hidden, base_key_value, preferred_element_typ...  14.4 us
    all_to_all x1, starting transfers between devices, shards(): lax.all_to_all(wanted.reshape(wide_count, 1), 'wide', split_axis=0, conca...  12 us
    ppermute x3, waiting for transfers between devices, narrow_sum(): cur = keep + lax.ppermute(send, 'narrow', pairs)  10.2 us
    ppermute x3, starting transfers between devices, narrow_sum(): other = lax.ppermute(cur, 'narrow', pairs)  8.68 us
    gather x1, local copies, waits for them, and re-layouts, shards(): needed = got[owners]  7.05 us
    all_to_all x1, waiting for transfers between devices, shards(): lax.all_to_all(wanted.reshape(wide_count, 1), 'wide', split_axis=0, conca...  6.67 us
  transfers between devices with their start and end apart: 9, of which 9 were waited for; matrix products, arithmetic and copies ran while one was open for 5% of the time, Pallas kernels for 0%

profile of v3, /device:TPU:1, one launch (start us, length us, event | category | flops | bytes accessed | tf_op | source)
XLA Modules:
  0.0 317.6 jit_solution(11632754377072928184)
XLA Ops:
  6.5 0.7 compare_select_fusion
  7.2 0.1 select_reduce_fusion
  7.3 0.7 copy.30
  8.0 12.0 %all-to-all-start = ((s32[32,1,1]{2,1,0:T(1,128)}), s32[32,1,1]{2,1,0:T(1,128)S(1)}, u32[]{:S(2)}, u32[]{:S(2)}) async-start(s32[32,1,1]{2,1,0:T(1,128)} %copy.30), calls=%async_computation | async-start | bytes 32768 | tf_op jit(solution)/shard_map/all_to_all | solution.py:60
  20.0 1.9 pad_maximum_fusion
  21.9 6.7 %all-to-all-done = s32[32,1,1]{2,1,0:T(1,128)S(1)} async-done(((s32[32,1,1]{2,1,0:T(1,128)}), s32[32,1,1]{2,1,0:T(1,128)S(1)}, u32[]{:S(2)}, u32[]{:S(2)}) %all-to-all-start) | async-done | bytes 160 | tf_op jit(solution)/shard_map/all_to_all | solution.py:60
  28.6 0.7 reduce
  29.2 5.4 %gather_fusion = bf16[32,1152,128]{2,1,0:T(8,128)(2,1)} fusion(bf16[8,1152,128]{2,1,0:T(8,128)(2,1)S(1)} %pad_maximum_fusion, s32[1024]{0:T(1024)S(1)} %pad_clamp_fusion.1), kind=kCustom, calls=%fused_computation | custom fusion | bytes 18874496 | tf_op jit(solution)/shard_map/gather | solution.py:66
  34.6 5.0 %all-to-all-start.1 = ((bf16[32,1152,128]{2,1,0:T(8,128)(2,1)}), bf16[32,1152,128]{2,1,0:T(8,128)(2,1)}, u32[]{:S(2)}, u32[]{:S(2)}) async-start(bf16[32,1152,128]{2,1,0:T(8,128)(2,1)} %gather_fusion), calls=%async_computation.1 | async-start | bytes 18874368 | tf_op jit(solution)/shard_map/all_to_all | solution.py:67
  39.6 0.0 reduce-scatter.2.cloned.1.call-start
  39.7 14.4 %convert_bitcast_fusion = bf16[8,2048,2,128]{1,3,2,0:T(8,128)(2,1)} fusion(bf16[2048,1024]{1,0:T(8,128)(2,1)} %param.6, bf16[1024,8,2,128]{3,2,1,0:T(2,128)(2,1)} %param.7), kind=kOutput, calls=%fused_computation.2 | convolution fusion | flops 8594128896 | bytes 16777216 | tf_op jit(solution)/shard_map/td,dhjc->htjc/dot_general | solution.py:69
  54.1 0.0 reduce-scatter.2.cloned.1.call-update
  54.2 57.2 %reduce-scatter.2.cloned.1.call-done = bf16[1,2048,2,128]{1,3,2,0:T(8,128)(2,1)} async-done(((bf16[8,2048,2,128]{1,3,2,0:T(8,128)(2,1)}), bf16[1,2048,2,128]{1,3,2,0:T(8,128)(2,1)}) %reduce-scatter.2.cloned.1.call-update) | async-done | bytes 1048592 | tf_op jit(solution)/shard_map/reduce_scatter | solution.py:72
  111.4 144.0 %all-to-all-done.1 = bf16[32,1152,128]{2,1,0:T(8,128)(2,1)} async-done(((bf16[32,1152,128]{2,1,0:T(8,128)(2,1)}), bf16[32,1152,128]{2,1,0:T(8,128)(2,1)}, u32[]{:S(2)}, u32[]{:S(2)}) %all-to-all-start.1) | async-done | bytes 9437216 | tf_op jit(solution)/shard_map/all_to_all | solution.py:67
  255.4 7.0 %gather_fusion.1 = bf16[16,1152,128]{2,1,0:T(8,128)(2,1)} fusion(bf16[32,1152,128]{2,1,0:T(8,128)(2,1)} %all-to-all-done.1, s32[1024]{0:T(1024)S(1)} %pad_clamp_fusion), kind=kCustom, calls=%fused_computation.1 | custom fusion | bytes 9437248 | tf_op jit(solution)/shard_map/gather | solution.py:78
  262.4 4.7 %fusion.4 = f32[16,128,128]{2,1,0:T(8,128)S(1)} fusion(bf16[16,128,1024]{2,1,0:T(8,128)(2,1)} %bitcast.51, bf16[16,1152,128]{2,1,0:T(8,128)(2,1)} %gather_fusion.1), kind=kOutput, calls=%fused_computation.10 | convolution fusion | flops 536870912 | bytes 9437184 | tf_op jit(solution)/shard_map/rtd,rdc->rtc/dot_general | solution.py:82
  267.1 0.0 copy-start
  267.1 0.1 slice_select_fusion
  267.2 0.2 copy.32
  267.4 1.5 collective-permute-start
  268.9 0.2 copy.33
  269.1 0.0 slice-start
  269.1 1.3 collective-permute-done
  270.5 0.1 add.66
  270.6 1.3 collective-permute-start.1
  271.9 6.3 %collective-permute-done.1 = f32[512,128]{0,1:T(8,128)S(1)} collective-permute-done((f32[512,128]{0,1:T(8,128)S(1)}, f32[512,128]{0,1:T(8,128)S(1)}, u32[]{:S(2)}, u32[]{:S(2)}) %collective-permute-start.1) | collective-permute-done | bytes 262176 | tf_op jit(solution)/shard_map/ppermute | solution.py:34
  278.2 0.1 select_add_fusion
  278.2 2.8 collective-permute-start.2
  281.1 2.6 collective-permute-done.2
  283.7 3.0 collective-permute-start.3
  286.7 0.0 copy-done
  286.7 1.9 collective-permute-done.3
  288.6 1.3 collective-permute-start.4
  289.9 0.1 convert_bitcast_fusion.1
  290.0 2.9 collective-permute-done.4
  292.9 0.1 maximum_select_fusion.1
  293.0 4.4 %collective-permute-start.5 = (bf16[1024,128]{0,1:T(8,128)(2,1)S(1)}, bf16[1024,128]{0,1:T(8,128)(2,1)S(1)}, u32[]{:S(2)}, u32[]{:S(2)}) collective-permute-start(bf16[1024,128]{0,1:T(8,128)(2,1)S(1)} %maximum_select_fusion.1), channel_id=1, source_target_pairs={{0,1},{1,0},{2,3},{3,2},{4,5},{5,4},{6,7},{7,6},{8,9},{9,8},{10,11... | collective-permute-start | bytes 786440 | tf_op jit(solution)/shard_map/ppermute | solution.py:39
  297.4 0.1 multiply_bitcast_fusion
  297.5 1.1 collective-permute-done.5
  298.5 0.1 fusion.14
  298.7 0.1 copy.38
  298.8 0.0 slice-done
  298.8 0.5 convolution_bitcast_fusion
  299.3 2.0 copy.35
  301.3 1.7 reshape.281
  303.0 1.5 convert_add_fusion
  304.5 0.1 slice_bitcast_fusion
  304.6 0.1 slice.96
  304.7 0.1 fusion.13
  304.8 3.9 %fusion.11 = bf16[1,2048,1,128]{1,3,2,0:T(8,128)(2,1)S(1)} fusion(f32[1,2048,1,64]{1,3,2,0:T(8,128)S(1)} %multiply_bitcast_fusion, f32[1,2048,1,64]{1,3,2,0:T(8,128)S(1)} %get-tuple-element.12, f32[1,2048,1,64]{1,3,2,0:T(8,128)S(1)} %get-tuple-element.11, f32[1,2048,2,128]{1,3,2,0:T(8,128)S(1)} %convert_add_fusion), kind=kLoop, calls=%fused_computation.17 | loop fusion | flops 1572864 | bytes 3145728 | tf_op jit(solution)/shard_map/convert
  308.7 0.1 pad_maximum_fusion.2
  308.8 2.0 copy.36
  (9 shorter events, 0.1 us)
Async XLA Ops:
  8.0 20.6 %all-to-all-start = ((s32[32,1,1]{2,1,0:T(1,128)}), s32[32,1,1]{2,1,0:T(1,128)S(1)}, u32[]{:S(2)}, u32[]{:S(2)}) async-start(s32[32,1,1]{2,1,0:T(1,128)} %copy.30), calls=%async_computation | async-start | bytes 32768 | tf_op jit(solution)/shard_map/all_to_all | solution.py:60
  34.6 220.7 %all-to-all-start.1 = ((bf16[32,1152,128]{2,1,0:T(8,128)(2,1)}), bf16[32,1152,128]{2,1,0:T(8,128)(2,1)}, u32[]{:S(2)}, u32[]{:S(2)}) async-start(bf16[32,1152,128]{2,1,0:T(8,128)(2,1)} %gather_fusion), calls=%async_computation.1 | async-start | bytes 18874368 | tf_op jit(solution)/shard_map/all_to_all | solution.py:67
  39.6 71.7 %reduce-scatter.2.cloned.1.call-start = ((), (), s32[]{:S(2)}) async-start(), calls=%async_computation.3 | async-start | bytes 9437184 | tf_op jit(solution)/shard_map/reduce_scatter | solution.py:72
  267.1 19.6 %copy-start = (s32[16]{0:T(128)S(1)}, s32[16]{0:T(128)}, u32[]{:S(2)}) copy-start(s32[16]{0:T(128)} %param.11) | copy-start | bytes 196
  267.4 3.0 collective-permute-start
  269.1 29.7 %slice-start = ((bf16[16,1152,128]{2,1,0:T(8,128)(2,1)}), bf16[16,128,128]{2,1,0:T(8,128)(2,1)S(1)}, s32[]{:S(2)}) async-start(bf16[16,1152,128]{2,1,0:T(8,128)(2,1)} %gather_fusion.1), calls=%async_computation.4 | async-start | bytes 1048576 | tf_op jit(solution)/shard_map/slice | solution.py:80
  270.6 7.6 %collective-permute-start.1 = (f32[512,128]{0,1:T(8,128)S(1)}, f32[512,128]{0,1:T(8,128)S(1)}, u32[]{:S(2)}, u32[]{:S(2)}) collective-permute-start(f32[512,128]{0,1:T(8,128)S(1)} %slice_select_fusion.2), channel_id=1, source_target_pairs={{0,2},{1,3},{2,0},{3,1},{4,6},{5,7},{6,4},{7,5},{8,10},{9,11},{10,... | collective-permute-start | bytes 786440 | tf_op jit(solution)/shard_map/ppermute | solution.py:34
  278.2 5.4 %collective-permute-start.2 = (f32[256,128]{0,1:T(8,128)S(1)}, f32[256,128]{0,1:T(8,128)S(1)}, u32[]{:S(2)}, u32[]{:S(2)}) collective-permute-start(f32[256,128]{0,1:T(8,128)S(1)} %slice_select_fusion.3), channel_id=1, source_target_pairs={{0,4},{1,5},{2,6},{3,7},{4,0},{5,1},{6,2},{7,3},{8,12},{9,13},{10,... | collective-permute-start | bytes 393224 | tf_op jit(solution)/shard_map/ppermute | solution.py:34
  283.7 4.9 %collective-permute-start.3 = (bf16[256,128]{0,1:T(8,128)(2,1)S(1)}, bf16[256,128]{0,1:T(8,128)(2,1)S(1)}, u32[]{:S(2)}, u32[]{:S(2)}) collective-permute-start(bf16[256,128]{0,1:T(8,128)(2,1)S(1)} %add_convert_fusion), channel_id=1, source_target_pairs={{0,4},{1,5},{2,6},{3,7},{4,0},{5,1},{6,2},{7,3},{8,12},{9,13},{10,... | collective-permute-start | bytes 196616 | tf_op jit(solution)/shard_map/ppermute | solution.py:39
  288.6 4.3 %collective-permute-start.4 = (bf16[512,128]{0,1:T(8,128)(2,1)S(1)}, bf16[512,128]{0,1:T(8,128)(2,1)S(1)}, u32[]{:S(2)}, u32[]{:S(2)}) collective-permute-start(bf16[512,128]{0,1:T(8,128)(2,1)S(1)} %maximum_select_fusion.2), channel_id=1, source_target_pairs={{0,2},{1,3},{2,0},{3,1},{4,6},{5,7},{6,4},{7,5},{8,10},{9,11},{10,... | collective-permute-start | bytes 393224 | tf_op jit(solution)/shard_map/ppermute | solution.py:39
  293.0 5.5 %collective-permute-start.5 = (bf16[1024,128]{0,1:T(8,128)(2,1)S(1)}, bf16[1024,128]{0,1:T(8,128)(2,1)S(1)}, u32[]{:S(2)}, u32[]{:S(2)}) collective-permute-start(bf16[1024,128]{0,1:T(8,128)(2,1)S(1)} %maximum_select_fusion.1), channel_id=1, source_target_pairs={{0,1},{1,0},{2,3},{3,2},{4,5},{5,4},{6,7},{7,6},{8,9},{9,8},{10,11... | collective-permute-start | bytes 786440 | tf_op jit(solution)/shard_map/ppermute | solution.py:39
Sparse Core Ops, SparseCore 0:
  54.3 57.0 reduce-scatter.1

commit v4 on v3

v4 whole, which is shorter than its diff:
```python
import jax
import jax.numpy as jnp
from jax import lax
from jax.experimental import pallas as pl
from jax.experimental.pallas import tpu as pltpu
from jax.sharding import PartitionSpec as P


THETA = 500000.0


def narrow_sum(v):
    count = lax.axis_size("narrow")
    me = lax.axis_index("narrow")
    bits = []
    bit = 1
    while bit < count:
        bits.append(bit)
        bit *= 2
    cur = v
    for bit in bits:
        half = cur.shape[0] // 2
        upper = (me & bit) > 0
        send = jnp.where(upper, cur[:half], cur[half:])
        keep = jnp.where(upper, cur[half:], cur[:half])
        pairs = [(i, i ^ bit) for i in range(count)]
        cur = keep + lax.ppermute(send, "narrow", pairs)
    cur = cur.astype(jnp.bfloat16)
    for bit in reversed(bits):
        upper = (me & bit) > 0
        pairs = [(i, i ^ bit) for i in range(count)]
        other = lax.ppermute(cur, "narrow", pairs)
        cur = jnp.where(
            upper, jnp.concatenate([other, cur]), jnp.concatenate([cur, other])
        )
    return cur


def shrink_body(owner_ref, rows_ref, maps_ref, out_ref):
    width = rows_ref.shape[1]
    out_ref[...] = jnp.dot(
        rows_ref[...], maps_ref[0, :width, :], preferred_element_type=jnp.float32
    )


def shrink(owners, hidden, got):
    requests = owners.shape[0]
    span_len = hidden.shape[0] // requests
    rows = got.shape[1]
    rank_two = got.shape[2]
    return pl.pallas_call(
        shrink_body,
        grid_spec=pltpu.PrefetchScalarGridSpec(
            num_scalar_prefetch=1,
            grid=(requests,),
            in_specs=[
                pl.BlockSpec((span_len, hidden.shape[1]), lambda r, own: (r, 0)),
                pl.BlockSpec((1, rows, rank_two), lambda r, own: (own[r], 0, 0)),
            ],
            out_specs=pl.BlockSpec((span_len, rank_two), lambda r, own: (r, 0)),
        ),
        out_shape=jax.ShapeDtypeStruct((hidden.shape[0], rank_two), jnp.float32),
    )(owners, hidden, got)


def finish_body(owner_ref, base_ref, shrunk_ref, up_ref, cos_ref, sin_ref, out_ref):
    rank_two = up_ref.shape[1]
    head_size = up_ref.shape[2]
    up = up_ref[0]
    row = lax.broadcasted_iota(jnp.int32, up.shape, 0)
    zero = jnp.zeros_like(up)
    keys_up = jnp.where(row < rank_two // 2, up, zero)
    values_up = jnp.where(row < rank_two // 2, zero, up)
    both_up = jnp.concatenate([keys_up, values_up], axis=1)
    delta = jnp.dot(shrunk_ref[...], both_up, preferred_element_type=jnp.float32)
    raw = base_ref[...].astype(jnp.float32) + delta
    keys = raw[:, :head_size]
    turned = pltpu.roll(keys, head_size // 2, 1)
    keys = keys * cos_ref[...] + turned * sin_ref[...]
    out_ref[...] = jnp.concatenate([keys, raw[:, head_size:]], axis=1).astype(out_ref.dtype)


def finish(owners, base, shrunk, got, cos, sin):
    requests = owners.shape[0]
    tokens = base.shape[0]
    span_len = tokens // requests
    rank_two = got.shape[2]
    up_block = got.shape[1] // rank_two - 1
    head_size = cos.shape[1]
    return pl.pallas_call(
        finish_body,
        grid_spec=pltpu.PrefetchScalarGridSpec(
            num_scalar_prefetch=1,
            grid=(requests,),
            in_specs=[
                pl.BlockSpec((span_len, base.shape[1]), lambda r, own: (r, 0)),
                pl.BlockSpec((span_len, rank_two), lambda r, own: (r, 0)),
                pl.BlockSpec(
                    (1, rank_two, rank_two), lambda r, own: (own[r], up_block, 0)
                ),
                pl.BlockSpec((span_len, head_size), lambda r, own: (r, 0)),
                pl.BlockSpec((span_len, head_size), lambda r, own: (r, 0)),
            ],
            out_specs=pl.BlockSpec((span_len, base.shape[1]), lambda r, own: (r, 0)),
        ),
        out_shape=jax.ShapeDtypeStruct(base.shape, jnp.bfloat16),
    )(owners, base, shrunk, got, cos, sin)


def rotation_tables(span_start, span_len, head_size):
    half_dim = head_size // 2
    positions = (
        (span_start[:, None] * span_len + jnp.arange(span_len, dtype=jnp.int32)[None, :])
        .reshape(-1)
        .astype(jnp.float32)
    )
    frequency = THETA ** (-(jnp.arange(half_dim, dtype=jnp.float32) * 2.0 / head_size))
    angles = positions[:, None] * frequency[None, :]
    cos = jnp.cos(angles)
    sin = jnp.sin(angles)
    return jnp.concatenate([cos, cos], axis=-1), jnp.concatenate([-sin, sin], axis=-1)


def shards(hidden, base_key_value, store_a, stored_up_maps, adapter_ids, span_start):
    wide_count = lax.axis_size("wide")
    stored = store_a.shape[0]
    requests = adapter_ids.shape[0]
    span_len = hidden.shape[0] // requests
    rank_two = store_a.shape[2]
    heads_here = stored_up_maps.shape[3]
    head_size = stored_up_maps.shape[4]

    owners = adapter_ids // stored
    matches = owners[None, :] == jnp.arange(wide_count, dtype=jnp.int32)[:, None]
    wanted = jnp.max(jnp.where(matches, adapter_ids % stored, 0), axis=1)
    chosen = lax.all_to_all(
        wanted.reshape(wide_count, 1), "wide", split_axis=0, concat_axis=0, tiled=True
    )[:, 0]

    up_rows = stored_up_maps.reshape(stored, rank_two * heads_here, head_size)
    packed = jnp.concatenate([store_a, up_rows], axis=1)
    reply = packed[chosen]
    got = lax.all_to_all(reply, "wide", split_axis=0, concat_axis=0, tiled=True)

    partials = jnp.einsum(
        "td,dhjc->htjc", hidden, base_key_value, preferred_element_type=jnp.float32
    ).astype(jnp.bfloat16)
    base_total_sum = lax.psum_scatter(
        partials, "narrow", scatter_dimension=0, tiled=True
    )
    got, base_total_sum = lax.optimization_barrier((got, base_total_sum))

    shrink_part = shrink(owners, hidden, got)
    shrunk = narrow_sum(shrink_part)
    cos, sin = rotation_tables(span_start, span_len, head_size)
    base_rows = base_total_sum.reshape(hidden.shape[0], 2 * head_size)
    joined = finish(owners, base_rows, shrunk, got, cos, sin)
    return joined.reshape(base_total_sum.shape)


def solution(mesh):
    placed = (
        P("wide", "narrow"),
        P("narrow", None, None, None),
        P("wide", "narrow", None),
        P("wide", None, None, "narrow", None),
        P("wide"),
        P("wide"),
    )
    return jax.shard_map(
        shards,
        mesh=mesh,
        in_specs=placed,
        out_specs=P("narrow", "wide", None, None),
        check_vma=False,
    )
```

time: 318 us -> 327 us (1.028)
  Pallas kernels: 0 us -> 24.1 us
  local copies, waits for them, and re-layouts: 19.5 us -> 9.55 us
  matrix products: 19.6 us -> 14.4 us
  waiting for transfers between devices: 224 us -> 220 us
    pallas_call x0 -> x2, Pallas kernels: none -> 24.1 us  [the longest x1 12.5 us: shrink(): pl.pallas_call(shrink_body, grid_spec=pltpu.PrefetchScalarGridSpec(num_sc...]
    gather x1 -> x0, local copies, waits for them, and re-layouts: 7.05 us -> none  [shards(): needed = got[owners]]
    dot_general x2 -> x0, matrix products: 5.2 us -> none  [the longest x1 4.71 us: shards(): jnp.einsum('rtd,rdc->rtc', request_rows, needed_a, preferred_element_type...]
    another operation x2 -> x0, other arithmetic: 3.98 us -> none
    ppermute x3, waiting for transfers between devices: 5.84 us -> 1.88 us  [narrow_sum(): other = lax.ppermute(cur, 'narrow', pairs)]
    neg x0 -> x1, other arithmetic: none -> 3.72 us  [rotation_tables(): -sin]
  transfers between devices with their start and end apart: 9 -> 9, of which waited for: 9 -> 7; matrix products, arithmetic and copies ran while one was open for 5% -> 7% of each run, Pallas kernels for 0% -> 0%
where the time goes in v4:
time: 327 us; the launch traced here: 325 us
  waiting for transfers between devices  220 us (67%)
  starting transfers between devices  30.9 us (9%)
  Pallas kernels  24.1 us (7%)
  matrix products  14.4 us (4%)
  between operations  13.5 us (4%)
  other arithmetic  12.7 us (4%)
  local copies, waits for them, and re-layouts  9.55 us (3%)
    all_to_all x1, waiting for transfers between devices, shards(): got = lax.all_to_all(reply, 'wide', split_axis=0, concat_axis=0, tiled=True)  144 us
    reduce_scatter x1, waiting for transfers between devices, shards(): lax.psum_scatter(partials, 'narrow', scatter_dimension=0, tiled=True)  57.2 us
    dot_general x1, matrix products, shards(): jnp.einsum('td,dhjc->htjc', hidden, base_key_value, preferred_element_typ...  14.4 us
    pallas_call x1, Pallas kernels, shrink(): pl.pallas_call(shrink_body, grid_spec=pltpu.PrefetchScalarGridSpec(num_sc...  12.5 us
    all_to_all x1, starting transfers between devices, shards(): lax.all_to_all(wanted.reshape(wide_count, 1), 'wide', split_axis=0, conca...  12 us
    pallas_call x1, Pallas kernels, finish(): pl.pallas_call(finish_body, grid_spec=pltpu.PrefetchScalarGridSpec(num_sc...  11.6 us
    ppermute x3, waiting for transfers between devices, narrow_sum(): cur = keep + lax.ppermute(send, 'narrow', pairs)  10.3 us
    ppermute x3, starting transfers between devices, narrow_sum(): other = lax.ppermute(cur, 'narrow', pairs)  8.2 us
  transfers between devices with their start and end apart: 9, of which 7 were waited for; matrix products, arithmetic and copies ran while one was open for 7% of the time, Pallas kernels for 0%

profile of v4, /device:TPU:1, one launch (start us, length us, event | category | flops | bytes accessed | tf_op | source)
XLA Modules:
  0.0 325.2 jit_solution(1782771427271259739)
XLA Ops:
  6.5 0.7 and_select_fusion
  7.2 0.0 copy-start.1
  7.2 0.1 select_reduce_fusion
  7.3 0.7 copy.15
  8.0 12.0 %all-to-all-start = ((s32[32,1,1]{2,1,0:T(1,128)}), s32[32,1,1]{2,1,0:T(1,128)S(1)}, u32[]{:S(2)}, u32[]{:S(2)}) async-start(s32[32,1,1]{2,1,0:T(1,128)} %copy.15), calls=%async_computation | async-start | bytes 32768 | tf_op jit(solution)/shard_map/all_to_all | solution.py:136
  20.0 1.9 pad_maximum_fusion
  21.9 6.7 %all-to-all-done = s32[32,1,1]{2,1,0:T(1,128)S(1)} async-done(((s32[32,1,1]{2,1,0:T(1,128)}), s32[32,1,1]{2,1,0:T(1,128)S(1)}, u32[]{:S(2)}, u32[]{:S(2)}) %all-to-all-start) | async-done | bytes 160 | tf_op jit(solution)/shard_map/all_to_all | solution.py:136
  28.6 0.7 reduce
  29.2 5.4 %gather_fusion = bf16[32,1152,128]{2,1,0:T(8,128)(2,1)} fusion(bf16[8,1152,128]{2,1,0:T(8,128)(2,1)S(1)} %pad_maximum_fusion, s32[1024]{0:T(1024)S(1)} %pad_clamp_fusion), kind=kCustom, calls=%fused_computation | custom fusion | bytes 18874496 | tf_op jit(solution)/shard_map/gather | solution.py:142
  34.6 0.0 copy-done.1
  34.6 5.0 %all-to-all-start.1 = ((bf16[32,1152,128]{2,1,0:T(8,128)(2,1)}), bf16[32,1152,128]{2,1,0:T(8,128)(2,1)}, u32[]{:S(2)}, u32[]{:S(2)}) async-start(bf16[32,1152,128]{2,1,0:T(8,128)(2,1)} %gather_fusion), calls=%async_computation.1 | async-start | bytes 18874368 | tf_op jit(solution)/shard_map/all_to_all | solution.py:143
  39.6 0.0 reduce-scatter.2.cloned.1.call-start
  39.7 14.4 %convert_bitcast_fusion = bf16[8,2048,2,128]{1,3,2,0:T(8,128)(2,1)} fusion(bf16[2048,1024]{1,0:T(8,128)(2,1)} %rows_ref.1, bf16[1024,8,2,128]{3,2,1,0:T(2,128)(2,1)} %param.7), kind=kOutput, calls=%fused_computation.1 | convolution fusion | flops 8594128896 | bytes 16777216 | tf_op jit(solution)/shard_map/td,dhjc->htjc/dot_general | solution.py:145
  54.1 0.0 reduce-scatter.2.cloned.1.call-update
  54.2 57.2 %reduce-scatter.2.cloned.1.call-done = bf16[1,2048,2,128]{1,3,2,0:T(8,128)(2,1)} async-done(((bf16[8,2048,2,128]{1,3,2,0:T(8,128)(2,1)}), bf16[1,2048,2,128]{1,3,2,0:T(8,128)(2,1)}) %reduce-scatter.2.cloned.1.call-update) | async-done | bytes 1048592 | tf_op jit(solution)/shard_map/reduce_scatter | solution.py:148
  111.4 144.0 %all-to-all-done.1.maps_ref.up_ref = bf16[32,1152,128]{2,1,0:T(8,128)(2,1)} async-done(((bf16[32,1152,128]{2,1,0:T(8,128)(2,1)}), bf16[32,1152,128]{2,1,0:T(8,128)(2,1)}, u32[]{:S(2)}, u32[]{:S(2)}) %all-to-all-start.1) | async-done | bytes 9437216 | tf_op jit(solution)/shard_map/all_to_all | solution.py:143
  255.4 12.5 %shard_map.64 = f32[2048,128]{1,0:T(8,128)} custom-call(s32[16]{0:T(128)} %copy-done.1, bf16[2048,1024]{1,0:T(8,128)(2,1)} %rows_ref.1, bf16[32,1152,128]{2,1,0:T(8,128)(2,1)} %all-to-all-done.1.maps_ref.up_ref), custom_call_target="tpu_custom_call" | custom-call | tf_op jit(solution)/shard_map/pallas_call | solution.py:51
  267.9 0.0 copy-start.2
  267.9 1.3 slice_select_fusion
  269.1 1.5 collective-permute-start
  270.6 1.5 collective-permute-done
  272.2 1.3 select_add_fusion
  273.5 1.3 collective-permute-start.1
  274.8 0.0 copy-done.2
  274.8 6.3 %collective-permute-done.1 = f32[512,128]{1,0:T(8,128)S(1)} collective-permute-done((f32[512,128]{1,0:T(8,128)S(1)}, f32[512,128]{1,0:T(8,128)S(1)}, u32[]{:S(2)}, u32[]{:S(2)}) %collective-permute-start.1) | collective-permute-done | bytes 262176 | tf_op jit(solution)/shard_map/ppermute | solution.py:27
  281.1 2.8 collective-permute-start.2
  284.0 0.1 convert_bitcast_fusion.1
  284.0 2.5 collective-permute-done.2
  286.6 2.8 collective-permute-start.3
  289.4 1.9 collective-permute-done.3
  291.3 0.0 copy-start
  291.3 1.5 collective-permute-start.4
  292.8 3.7 %fusion.2 = (f32[2048,64]{1,0:T(8,128)S(1)}, f32[2048,64]{1,0:T(8,128)S(1)}, f32[2048,64]{1,0:T(8,128)S(1)}) fusion(f32[64]{0:T(128)S(1)} %negate_power_fusion, f32[2048]{0:T(1024)S(1)} %convert_bitcast_fusion.1), kind=kLoop, calls=%fused_computation.12 | loop fusion | flops 262144 | bytes 1581312 | tf_op jit(solution)/shard_map/neg | solution.py:121
  296.5 0.0 collective-permute-done.4
  296.5 0.1 maximum_select_fusion.1
  296.6 3.9 %collective-permute-start.5 = (bf16[1024,128]{1,0:T(8,128)(2,1)S(1)}, bf16[1024,128]{1,0:T(8,128)(2,1)S(1)}, u32[]{:S(2)}, u32[]{:S(2)}) collective-permute-start(bf16[1024,128]{1,0:T(8,128)(2,1)S(1)} %maximum_select_fusion.1), channel_id=1, source_target_pairs={{0,1},{1,0},{2,3},{3,2},{4,5},{5,4},{6,7},{7,6},{8,9},{9,8},{10,11... | collective-permute-start | bytes 786440 | tf_op jit(solution)/shard_map/ppermute | solution.py:32
  300.5 1.9 pad_maximum_fusion.1
  302.4 0.0 copy-done
  302.4 1.3 copy.19.base_ref
  303.7 0.0 collective-permute-done.5
  303.7 0.9 maximum_select_fusion.shrunk_ref
  304.7 11.6 %shard_map.65 = bf16[2048,256]{1,0:T(8,128)(2,1)} custom-call(s32[16]{0:T(128)} %copy-done.1, bf16[2048,256]{1,0:T(8,128)(2,1)} %copy.19.base_ref, bf16[2048,128]{1,0:T(8,128)(2,1)} %maximum_select_fusion.shrunk_ref, bf16[32,1152,128]{2,1,0:T(8,128)(2,1)} %all-to-all-done.1.maps_ref.up_ref, f32[2048,128]{1,0:T(8,128)} %get-tuple-element.14.cos_ref, ...), custom_call_target="tpu_custom_call" | custom-call | tf_op jit(solution)/shard_map/pallas_call | solution.py:90
  316.3 2.1 reshape.66
  (9 shorter events, 0.2 us)
Async XLA Ops:
  7.2 27.4 %copy-start.1 = (s32[16]{0:T(128)}, s32[16]{0:T(128)S(1)}, u32[]{:S(2)}) copy-start(s32[16]{0:T(128)S(1)} %get-tuple-element.13.owner_ref) | copy-start | bytes 196
  8.0 20.6 %all-to-all-start = ((s32[32,1,1]{2,1,0:T(1,128)}), s32[32,1,1]{2,1,0:T(1,128)S(1)}, u32[]{:S(2)}, u32[]{:S(2)}) async-start(s32[32,1,1]{2,1,0:T(1,128)} %copy.15), calls=%async_computation | async-start | bytes 32768 | tf_op jit(solution)/shard_map/all_to_all | solution.py:136
  34.6 220.7 %all-to-all-start.1 = ((bf16[32,1152,128]{2,1,0:T(8,128)(2,1)}), bf16[32,1152,128]{2,1,0:T(8,128)(2,1)}, u32[]{:S(2)}, u32[]{:S(2)}) async-start(bf16[32,1152,128]{2,1,0:T(8,128)(2,1)} %gather_fusion), calls=%async_computation.1 | async-start | bytes 18874368 | tf_op jit(solution)/shard_map/all_to_all | solution.py:143
  39.6 71.7 %reduce-scatter.2.cloned.1.call-start = ((), (), s32[]{:S(2)}) async-start(), calls=%async_computation.3 | async-start | bytes 9437184 | tf_op jit(solution)/shard_map/reduce_scatter | solution.py:148
  267.9 6.9 %copy-start.2 = (s32[16]{0:T(128)S(1)}, s32[16]{0:T(128)}, u32[]{:S(2)}) copy-start(s32[16]{0:T(128)} %param.11) | copy-start | bytes 196
  269.1 3.0 collective-permute-start
  273.5 7.6 %collective-permute-start.1 = (f32[512,128]{1,0:T(8,128)S(1)}, f32[512,128]{1,0:T(8,128)S(1)}, u32[]{:S(2)}, u32[]{:S(2)}) collective-permute-start(f32[512,128]{1,0:T(8,128)S(1)} %slice_select_fusion.1), channel_id=1, source_target_pairs={{0,2},{1,3},{2,0},{3,1},{4,6},{5,7},{6,4},{7,5},{8,10},{9,11},{10,... | collective-permute-start | bytes 786440 | tf_op jit(solution)/shard_map/ppermute | solution.py:27
  281.1 5.4 %collective-permute-start.2 = (f32[256,128]{1,0:T(8,128)S(1)}, f32[256,128]{1,0:T(8,128)S(1)}, u32[]{:S(2)}, u32[]{:S(2)}) collective-permute-start(f32[256,128]{1,0:T(8,128)S(1)} %slice_select_fusion.2), channel_id=1, source_target_pairs={{0,4},{1,5},{2,6},{3,7},{4,0},{5,1},{6,2},{7,3},{8,12},{9,13},{10,... | collective-permute-start | bytes 393224 | tf_op jit(solution)/shard_map/ppermute | solution.py:27
  286.6 4.7 %collective-permute-start.3 = (bf16[256,128]{1,0:T(8,128)(2,1)S(1)}, bf16[256,128]{1,0:T(8,128)(2,1)S(1)}, u32[]{:S(2)}, u32[]{:S(2)}) collective-permute-start(bf16[256,128]{1,0:T(8,128)(2,1)S(1)} %add_convert_fusion), channel_id=1, source_target_pairs={{0,4},{1,5},{2,6},{3,7},{4,0},{5,1},{6,2},{7,3},{8,12},{9,13},{10,... | collective-permute-start | bytes 196616 | tf_op jit(solution)/shard_map/ppermute | solution.py:32
  291.3 11.1 %copy-start = (bf16[1,2048,2,128]{1,3,2,0:T(8,128)(2,1)S(1)}, bf16[1,2048,2,128]{1,3,2,0:T(8,128)(2,1)}, u32[]{:S(2)}) copy-start(bf16[1,2048,2,128]{1,3,2,0:T(8,128)(2,1)} %reduce-scatter.2.cloned.1.call-done) | copy-start | bytes 3145732
  291.3 5.2 %collective-permute-start.4 = (bf16[512,128]{1,0:T(8,128)(2,1)S(1)}, bf16[512,128]{1,0:T(8,128)(2,1)S(1)}, u32[]{:S(2)}, u32[]{:S(2)}) collective-permute-start(bf16[512,128]{1,0:T(8,128)(2,1)S(1)} %maximum_select_fusion.2), channel_id=1, source_target_pairs={{0,2},{1,3},{2,0},{3,1},{4,6},{5,7},{6,4},{7,5},{8,10},{9,11},{10,... | collective-permute-start | bytes 393224 | tf_op jit(solution)/shard_map/ppermute | solution.py:32
  296.6 7.1 %collective-permute-start.5 = (bf16[1024,128]{1,0:T(8,128)(2,1)S(1)}, bf16[1024,128]{1,0:T(8,128)(2,1)S(1)}, u32[]{:S(2)}, u32[]{:S(2)}) collective-permute-start(bf16[1024,128]{1,0:T(8,128)(2,1)S(1)} %maximum_select_fusion.1), channel_id=1, source_target_pairs={{0,1},{1,0},{2,3},{3,2},{4,5},{5,4},{6,7},{7,6},{8,9},{9,8},{10,11... | collective-permute-start | bytes 786440 | tf_op jit(solution)/shard_map/ppermute | solution.py:32
Sparse Core Ops, SparseCore 0:
  54.3 57.0 reduce-scatter.1

commit v5 on v3

--- a/solution.py
+++ b/solution.py
@@ -66,36 +66,45 @@
     reply = packed[chosen]
     got = lax.all_to_all(reply, "wide", split_axis=0, concat_axis=0, tiled=True)
 
-    partials = jnp.einsum(
-        "td,dhjc->htjc", hidden, base_key_value, preferred_element_type=jnp.float32
-    ).astype(jnp.bfloat16)
+    tokens = hidden.shape[0]
+    heads = base_key_value.shape[1]
+    flat_w = base_key_value.reshape(width, heads * 2 * head_size)
+    partials = jnp.dot(hidden, flat_w, preferred_element_type=jnp.float32)
+    partials = partials.astype(jnp.bfloat16).reshape(tokens, heads, 2 * head_size)
+    partials = partials.transpose(1, 0, 2)
     base_total_sum = lax.psum_scatter(
         partials, "narrow", scatter_dimension=0, tiled=True
     )
     got, base_total_sum = lax.optimization_barrier((got, base_total_sum))
-    base_total_sum = base_total_sum.astype(jnp.float32)
 
     needed = got[owners]
     needed_a = needed[:, :width]
-    needed_b = needed[:, width:].reshape(requests, 2, rank, heads_here, head_size)
+    up = needed[:, width:]
     request_rows = hidden.reshape(requests, span_len, hidden.shape[1])
     shrink_part = jnp.einsum(
         "rtd,rdc->rtc", request_rows, needed_a, preferred_element_type=jnp.float32
     )
     shrunk = narrow_sum(shrink_part.reshape(requests * span_len, rank_two))
-    shrunk_split = shrunk.reshape(requests, span_len, 2, rank)
+    row = lax.broadcasted_iota(jnp.int32, up.shape, 1)
+    zero = jnp.zeros_like(up)
+    both_up = jnp.concatenate(
+        [jnp.where(row < rank, up, zero), jnp.where(row < rank, zero, up)], axis=2
+    )
     delta = jnp.einsum(
-        "rtjk,rjkhc->hrtjc", shrunk_split, needed_b, preferred_element_type=jnp.float32
-    )
-    raw = base_total_sum + delta.reshape(base_total_sum.shape)
+        "rtk,rkc->rtc",
+        shrunk.reshape(requests, span_len, rank_two),
+        both_up,
+        preferred_element_type=jnp.float32,
+    ).reshape(tokens, 2 * head_size)
+    raw = base_total_sum.reshape(tokens, 2 * head_size).astype(jnp.float32) + delta
     positions = (
         (span_start[:, None] * span_len + jnp.arange(span_len, dtype=jnp.int32)[None, :])
         .reshape(-1)
         .astype(jnp.float32)
     )
-    keys_turned = jax.vmap(lambda head_keys: rotate_keys(head_keys, positions))(raw[:, :, 0, :])
-    joined = jnp.stack([keys_turned, raw[:, :, 1, :]], axis=2)
-    return joined.astype(jnp.bfloat16)
+    keys_turned = rotate_keys(raw[:, :head_size], positions)
+    joined = jnp.concatenate([keys_turned, raw[:, head_size:]], axis=1)
+    return joined.astype(jnp.bfloat16).reshape(base_total_sum.shape[0], tokens, 2, head_size)
 
 
 def solution(mesh):

time: 318 us -> 324 us (1.019)
  the two profiles are of different devices: /device:TPU:1 before, /device:TPU:127 now
where the time goes in v5:
time: 324 us; the launch traced here: 323 us
  waiting for transfers between devices  225 us (69%)
  starting transfers between devices  29.4 us (9%)
  local copies, waits for them, and re-layouts  24.9 us (8%)
  matrix products  19.1 us (6%)
  between operations  13.6 us (4%)
  other arithmetic  11 us (3%)
    all_to_all x1, waiting for transfers between devices, shards(): got = lax.all_to_all(reply, 'wide', split_axis=0, concat_axis=0, tiled=True)  150 us
    reduce_scatter x1, waiting for transfers between devices, shards(): lax.psum_scatter(partials, 'narrow', scatter_dimension=0, tiled=True)  56.3 us
    dot_general x1, matrix products, shards(): partials = jnp.dot(hidden, flat_w, preferred_element_type=jnp.float32)  14 us
    ppermute x3, waiting for transfers between devices, narrow_sum(): cur = keep + lax.ppermute(send, 'narrow', pairs)  12.7 us
    all_to_all x1, starting transfers between devices, shards(): lax.all_to_all(wanted.reshape(wide_count, 1), 'wide', split_axis=0, conca...  9.56 us
    all_to_all x1, starting transfers between devices, shards(): got = lax.all_to_all(reply, 'wide', split_axis=0, concat_axis=0, tiled=True)  9.29 us
    reshape x1, local copies, waits for them, and re-layouts, shards(): flat_w = base_key_value.reshape(width, heads * 2 * head_size)  7.81 us
    ppermute x3, starting transfers between devices, narrow_sum(): other = lax.ppermute(cur, 'narrow', pairs)  7.17 us
  transfers between devices with their start and end apart: 9, of which 7 were waited for; matrix products, arithmetic and copies ran while one was open for 8% of the time, Pallas kernels for 0%

profile of v5, /device:TPU:127, one launch (start us, length us, event | category | flops | bytes accessed | tf_op | source)
XLA Modules:
  0.0 323.4 jit_solution(11461355111260802430)
XLA Ops:
  6.5 0.7 compare_select_fusion
  7.2 0.1 select_reduce_fusion
  7.3 0.7 copy.15
  8.0 9.6 %all-to-all-start = ((s32[32,1,1]{2,1,0:T(1,128)}), s32[32,1,1]{2,1,0:T(1,128)S(1)}, u32[]{:S(2)}, u32[]{:S(2)}) async-start(s32[32,1,1]{2,1,0:T(1,128)} %copy.15), calls=%async_computation | async-start | bytes 32768 | tf_op jit(solution)/shard_map/all_to_all | solution.py:60
  17.5 1.9 pad_maximum_fusion
  19.4 7.8 %reshape.98 = bf16[1024,2048]{1,0:T(8,128)(2,1)} reshape(bf16[1024,8,2,128]{3,2,1,0:T(2,128)(2,1)} %param.7) | data formatting | bytes 8388608 | tf_op jit(solution)/shard_map/reshape | solution.py:71
  27.2 0.0 all-to-all-done
  27.2 0.7 reduce
  27.9 5.4 %gather_fusion = bf16[32,1152,128]{2,1,0:T(8,128)(2,1)} fusion(bf16[8,1152,128]{2,1,0:T(8,128)(2,1)S(1)} %pad_maximum_fusion, s32[1024]{0:T(1024)S(1)} %pad_clamp_fusion.1), kind=kCustom, calls=%fused_computation | custom fusion | bytes 18874496 | tf_op jit(solution)/shard_map/gather | solution.py:66
  33.3 9.3 %all-to-all-start.1 = ((bf16[32,1152,128]{2,1,0:T(8,128)(2,1)}), bf16[32,1152,128]{2,1,0:T(8,128)(2,1)}, u32[]{:S(2)}, u32[]{:S(2)}) async-start(bf16[32,1152,128]{2,1,0:T(8,128)(2,1)} %gather_fusion), calls=%async_computation.1 | async-start | bytes 18874368 | tf_op jit(solution)/shard_map/all_to_all | solution.py:67
  42.6 0.0 reduce-scatter.2.cloned.1.call-start
  42.7 14.0 %convolution_convert_fusion = bf16[2048,2048]{0,1:T(8,128)(2,1)} fusion(bf16[2048,1024]{1,0:T(8,128)(2,1)} %param.6, bf16[1024,2048]{1,0:T(8,128)(2,1)} %reshape.98), kind=kOutput, calls=%fused_computation.2 | convolution fusion | flops 8594128896 | bytes 16777216 | tf_op jit(solution)/shard_map/dot_general | solution.py:72
  56.6 0.0 reduce-scatter.2.cloned.1.call-update
  56.7 56.3 %reduce-scatter.2.cloned.1.call-done = bf16[1,2048,256]{1,2,0:T(8,128)(2,1)} async-done(((bf16[8,2048,256]{1,2,0:T(8,128)(2,1)}), bf16[1,2048,256]{1,2,0:T(8,128)(2,1)}) %reduce-scatter.2.cloned.1.call-update) | async-done | bytes 1048592 | tf_op jit(solution)/shard_map/reduce_scatter | solution.py:75
  113.0 149.7 %all-to-all-done.1 = bf16[32,1152,128]{2,1,0:T(8,128)(2,1)} async-done(((bf16[32,1152,128]{2,1,0:T(8,128)(2,1)}), bf16[32,1152,128]{2,1,0:T(8,128)(2,1)}, u32[]{:S(2)}, u32[]{:S(2)}) %all-to-all-start.1) | async-done | bytes 9437216 | tf_op jit(solution)/shard_map/all_to_all | solution.py:67
  262.7 7.0 %gather_fusion.1 = bf16[16,1152,128]{2,1,0:T(8,128)(2,1)} fusion(bf16[32,1152,128]{2,1,0:T(8,128)(2,1)} %all-to-all-done.1, s32[1024]{0:T(1024)S(1)} %pad_clamp_fusion), kind=kCustom, calls=%fused_computation.1 | custom fusion | bytes 9437248 | tf_op jit(solution)/shard_map/gather | solution.py:80
  269.8 4.7 %fusion.2 = f32[16,128,128]{2,1,0:T(8,128)S(1)} fusion(bf16[16,128,1024]{2,1,0:T(8,128)(2,1)} %bitcast.34, bf16[16,1152,128]{2,1,0:T(8,128)(2,1)} %gather_fusion.1), kind=kOutput, calls=%fused_computation.7 | convolution fusion | flops 536870912 | bytes 9437184 | tf_op jit(solution)/shard_map/rtd,rdc->rtc/dot_general | solution.py:84
  274.5 0.0 copy-start.1
  274.5 0.1 slice_select_fusion.1
  274.6 1.5 collective-permute-start
  276.1 1.5 collective-permute-done
  277.7 0.1 bitcast_add_fusion
  277.8 0.6 collective-permute-start.1
  278.4 6.9 %collective-permute-done.1 = f32[512,128]{1,0:T(8,128)S(1)} collective-permute-done((f32[512,128]{1,0:T(8,128)S(1)}, f32[512,128]{1,0:T(8,128)S(1)}, u32[]{:S(2)}, u32[]{:S(2)}) %collective-permute-start.1) | collective-permute-done | bytes 262176 | tf_op jit(solution)/shard_map/ppermute | solution.py:34
  285.4 1.2 collective-permute-start.2
  286.6 0.0 copy-done.1
  286.6 4.2 %collective-permute-done.2 = f32[256,128]{1,0:T(8,128)S(1)} collective-permute-done((f32[256,128]{1,0:T(8,128)S(1)}, f32[256,128]{1,0:T(8,128)S(1)}, u32[]{:S(2)}, u32[]{:S(2)}) %collective-permute-start.2) | collective-permute-done | bytes 131104 | tf_op jit(solution)/shard_map/ppermute | solution.py:34
  290.8 1.4 collective-permute-start.3
  292.2 0.1 convert_bitcast_fusion
  292.3 3.4 %collective-permute-done.3 = bf16[256,128]{1,0:T(8,128)(2,1)S(1)} collective-permute-done((bf16[256,128]{1,0:T(8,128)(2,1)S(1)}, bf16[256,128]{1,0:T(8,128)(2,1)S(1)}, u32[]{:S(2)}, u32[]{:S(2)}) %collective-permute-start.3) | collective-permute-done | bytes 65568 | tf_op jit(solution)/shard_map/ppermute | solution.py:39
  295.8 0.6 collective-permute-start.4
  296.4 3.3 %collective-permute-done.4 = bf16[512,128]{1,0:T(8,128)(2,1)S(1)} collective-permute-done((bf16[512,128]{1,0:T(8,128)(2,1)S(1)}, bf16[512,128]{1,0:T(8,128)(2,1)S(1)}, u32[]{:S(2)}, u32[]{:S(2)}) %collective-permute-start.4) | collective-permute-done | bytes 131104 | tf_op jit(solution)/shard_map/ppermute | solution.py:39
  299.7 0.1 maximum_select_fusion.1
  299.8 5.1 %collective-permute-start.5 = (bf16[1024,128]{1,0:T(8,128)(2,1)S(1)}, bf16[1024,128]{1,0:T(8,128)(2,1)S(1)}, u32[]{:S(2)}, u32[]{:S(2)}) collective-permute-start(bf16[1024,128]{1,0:T(8,128)(2,1)S(1)} %maximum_select_fusion.1), channel_id=1, source_target_pairs={{0,1},{1,0},{2,3},{3,2},{4,5},{5,4},{6,7},{7,6},{8,9},{9,8},{10,11... | collective-permute-start | bytes 786440 | tf_op jit(solution)/shard_map/ppermute | solution.py:39
  304.9 1.2 broadcast_select_fusion.1
  306.1 0.0 collective-permute-done.5
  306.1 0.1 maximum_select_fusion
  306.3 0.0 copy-start
  306.3 0.4 fusion.7
  306.7 1.9 copy.16
  308.5 0.0 copy-done
  308.6 1.9 convert_add_fusion
  310.4 0.1 slice.100
  310.5 0.1 slice_negate_fusion
  310.6 3.9 %fusion.6 = bf16[2048,128]{0,1:T(8,128)(2,1)S(1)} fusion(f32[2048,256]{0,1:T(8,128)S(1)} %convert_add_fusion, f32[2048,64]{0,1:T(8,128)S(1)} %get-tuple-element.18, f32[2048,64]{0,1:T(8,128)S(1)} %get-tuple-element.14, f32[2048,64]{0,1:T(8,128)S(1)} %get-tuple-element.13), kind=kLoop, calls=%fused_computation.11 | loop fusion | flops 1572864 | bytes 3145728 | tf_op jit(solution)/shard_map/convert.1
  314.5 0.1 pad_maximum_fusion.2
  314.6 2.0 copy.18
  (11 shorter events, 0.2 us)
Async XLA Ops:
  8.0 19.2 %all-to-all-start = ((s32[32,1,1]{2,1,0:T(1,128)}), s32[32,1,1]{2,1,0:T(1,128)S(1)}, u32[]{:S(2)}, u32[]{:S(2)}) async-start(s32[32,1,1]{2,1,0:T(1,128)} %copy.15), calls=%async_computation | async-start | bytes 32768 | tf_op jit(solution)/shard_map/all_to_all | solution.py:60
  33.3 229.4 %all-to-all-start.1 = ((bf16[32,1152,128]{2,1,0:T(8,128)(2,1)}), bf16[32,1152,128]{2,1,0:T(8,128)(2,1)}, u32[]{:S(2)}, u32[]{:S(2)}) async-start(bf16[32,1152,128]{2,1,0:T(8,128)(2,1)} %gather_fusion), calls=%async_computation.1 | async-start | bytes 18874368 | tf_op jit(solution)/shard_map/all_to_all | solution.py:67
  42.6 70.4 %reduce-scatter.2.cloned.1.call-start = ((), (), s32[]{:S(2)}) async-start(), calls=%async_computation.3 | async-start | bytes 9437184 | tf_op jit(solution)/shard_map/reduce_scatter | solution.py:75
  274.5 12.1 %copy-start.1 = (s32[16]{0:T(128)S(1)}, s32[16]{0:T(128)}, u32[]{:S(2)}) copy-start(s32[16]{0:T(128)} %param.11) | copy-start | bytes 196
  274.6 3.1 collective-permute-start
  277.8 7.6 %collective-permute-start.1 = (f32[512,128]{1,0:T(8,128)S(1)}, f32[512,128]{1,0:T(8,128)S(1)}, u32[]{:S(2)}, u32[]{:S(2)}) collective-permute-start(f32[512,128]{1,0:T(8,128)S(1)} %slice_select_fusion.2), channel_id=1, source_target_pairs={{0,2},{1,3},{2,0},{3,1},{4,6},{5,7},{6,4},{7,5},{8,10},{9,11},{10,... | collective-permute-start | bytes 786440 | tf_op jit(solution)/shard_map/ppermute | solution.py:34
  285.4 5.4 %collective-permute-start.2 = (f32[256,128]{1,0:T(8,128)S(1)}, f32[256,128]{1,0:T(8,128)S(1)}, u32[]{:S(2)}, u32[]{:S(2)}) collective-permute-start(f32[256,128]{1,0:T(8,128)S(1)} %slice_select_fusion.3), channel_id=1, source_target_pairs={{0,4},{1,5},{2,6},{3,7},{4,0},{5,1},{6,2},{7,3},{8,12},{9,13},{10,... | collective-permute-start | bytes 393224 | tf_op jit(solution)/shard_map/ppermute | solution.py:34
  290.8 4.9 %collective-permute-start.3 = (bf16[256,128]{1,0:T(8,128)(2,1)S(1)}, bf16[256,128]{1,0:T(8,128)(2,1)S(1)}, u32[]{:S(2)}, u32[]{:S(2)}) collective-permute-start(bf16[256,128]{1,0:T(8,128)(2,1)S(1)} %add_convert_fusion), channel_id=1, source_target_pairs={{0,4},{1,5},{2,6},{3,7},{4,0},{5,1},{6,2},{7,3},{8,12},{9,13},{10,... | collective-permute-start | bytes 196616 | tf_op jit(solution)/shard_map/ppermute | solution.py:39
  295.8 3.9 %collective-permute-start.4 = (bf16[512,128]{1,0:T(8,128)(2,1)S(1)}, bf16[512,128]{1,0:T(8,128)(2,1)S(1)}, u32[]{:S(2)}, u32[]{:S(2)}) collective-permute-start(bf16[512,128]{1,0:T(8,128)(2,1)S(1)} %maximum_select_fusion.2), channel_id=1, source_target_pairs={{0,2},{1,3},{2,0},{3,1},{4,6},{5,7},{6,4},{7,5},{8,10},{9,11},{10,... | collective-permute-start | bytes 393224 | tf_op jit(solution)/shard_map/ppermute | solution.py:39
  299.8 6.3 %collective-permute-start.5 = (bf16[1024,128]{1,0:T(8,128)(2,1)S(1)}, bf16[1024,128]{1,0:T(8,128)(2,1)S(1)}, u32[]{:S(2)}, u32[]{:S(2)}) collective-permute-start(bf16[1024,128]{1,0:T(8,128)(2,1)S(1)} %maximum_select_fusion.1), channel_id=1, source_target_pairs={{0,1},{1,0},{2,3},{3,2},{4,5},{5,4},{6,7},{7,6},{8,9},{9,8},{10,11... | collective-permute-start | bytes 786440 | tf_op jit(solution)/shard_map/ppermute | solution.py:39
  306.3 2.3 copy-start
Sparse Core Ops, SparseCore 0:
  56.8 56.1 reduce-scatter.1

commit v6 on v5

--- a/solution.py
+++ b/solution.py
@@ -43,6 +43,24 @@
     return cur
 
 
+def narrow_scatter(v):
+    count = lax.axis_size("narrow")
+    me = lax.axis_index("narrow")
+    cur = v
+    bit = 1
+    while bit < count:
+        pairs = [(i, i ^ bit) for i in range(count)]
+        halves = cur.reshape(cur.shape[0] // 2, 2, *cur.shape[1:])
+        keep = (me // bit) % 2
+        mine = lax.dynamic_index_in_dim(halves, keep, axis=1, keepdims=False)
+        theirs = lax.dynamic_index_in_dim(halves, 1 - keep, axis=1, keepdims=False)
+        cur = mine.astype(jnp.float32) + lax.ppermute(theirs, "narrow", pairs).astype(
+            jnp.float32
+        )
+        bit *= 2
+    return cur
+
+
 def shards(hidden, base_key_value, store_a, stored_up_maps, adapter_ids, span_start):
     wide_count = lax.axis_size("wide")
     stored = store_a.shape[0]
@@ -72,9 +90,7 @@
     partials = jnp.dot(hidden, flat_w, preferred_element_type=jnp.float32)
     partials = partials.astype(jnp.bfloat16).reshape(tokens, heads, 2 * head_size)
     partials = partials.transpose(1, 0, 2)
-    base_total_sum = lax.psum_scatter(
-        partials, "narrow", scatter_dimension=0, tiled=True
-    )
+    base_total_sum = narrow_scatter(partials)
     got, base_total_sum = lax.optimization_barrier((got, base_total_sum))
 
     needed = got[owners]

time: 324 us -> 301 us (0.929)
  the two profiles are of different devices: /device:TPU:127 before, /device:TPU:1 now
where the time goes in v6:
time: 301 us; the launch traced here: 300 us
  waiting for transfers between devices  178 us (59%)
  local copies, waits for them, and re-layouts  43.6 us (14%)
  starting transfers between devices  37.3 us (12%)
  other arithmetic  23.8 us (8%)
  matrix products  17.1 us (6%)
    ppermute x3, waiting for transfers between devices, narrow_scatter(): lax.ppermute(theirs, 'narrow', pairs).astype(jnp.float32)  137 us
    all_to_all x1, waiting for transfers between devices, shards(): got = lax.all_to_all(reply, 'wide', split_axis=0, concat_axis=0, tiled=True)  19 us
    unnamed x8, local copies, waits for them, and re-layouts  14.9 us
    all_to_all x1, starting transfers between devices, shards(): lax.all_to_all(wanted.reshape(wide_count, 1), 'wide', split_axis=0, conca...  12 us
    dot_general x1, matrix products, shards(): partials = jnp.dot(hidden, flat_w, preferred_element_type=jnp.float32)  12 us
    add x3, other arithmetic, narrow_scatter(): mine.astype(jnp.float32)  11.9 us
    ppermute x3, waiting for transfers between devices, narrow_sum(): cur = keep + lax.ppermute(send, 'narrow', pairs)  10.5 us
    ppermute x3, starting transfers between devices, narrow_sum(): other = lax.ppermute(cur, 'narrow', pairs)  8.51 us
  transfers between devices with their start and end apart: 11, of which 10 were waited for; matrix products, arithmetic and copies ran while one was open for 17% of the time, Pallas kernels for 0%

profile of v6, /device:TPU:1, one launch (start us, length us, event | category | flops | bytes accessed | tf_op | source)
XLA Modules:
  0.0 300.4 jit_solution(14179022548693092466)
XLA Ops:
  0.0 0.7 compare_select_fusion
  0.7 0.1 select_reduce_fusion
  0.8 0.7 copy.15
  1.4 12.0 %all-to-all-start = ((s32[32,1,1]{2,1,0:T(1,128)}), s32[32,1,1]{2,1,0:T(1,128)S(1)}, u32[]{:S(2)}, u32[]{:S(2)}) async-start(s32[32,1,1]{2,1,0:T(1,128)} %copy.15), calls=%async_computation | async-start | bytes 32768 | tf_op jit(solution)/shard_map/all_to_all | solution.py:78
  13.5 1.9 pad_maximum_fusion
  15.3 6.7 %all-to-all-done = s32[32,1,1]{2,1,0:T(1,128)S(1)} async-done(((s32[32,1,1]{2,1,0:T(1,128)}), s32[32,1,1]{2,1,0:T(1,128)S(1)}, u32[]{:S(2)}, u32[]{:S(2)}) %all-to-all-start) | async-done | bytes 160 | tf_op jit(solution)/shard_map/all_to_all | solution.py:78
  22.0 0.7 reduce
  22.7 5.4 %gather_fusion = bf16[32,1152,128]{2,1,0:T(8,128)(2,1)} fusion(bf16[8,1152,128]{2,1,0:T(8,128)(2,1)S(1)} %pad_maximum_fusion, s32[1024]{0:T(1024)S(1)} %pad_clamp_fusion.1), kind=kCustom, calls=%fused_computation | custom fusion | bytes 18874496 | tf_op jit(solution)/shard_map/gather | solution.py:84
  28.1 5.0 %all-to-all-start.1 = ((bf16[32,1152,128]{2,1,0:T(8,128)(2,1)}), bf16[32,1152,128]{2,1,0:T(8,128)(2,1)}, u32[]{:S(2)}, u32[]{:S(2)}) async-start(bf16[32,1152,128]{2,1,0:T(8,128)(2,1)} %gather_fusion), calls=%async_computation.1 | async-start | bytes 18874368 | tf_op jit(solution)/shard_map/all_to_all | solution.py:85
  33.1 7.8 %reshape.111 = bf16[1024,2048]{1,0:T(8,128)(2,1)} reshape(bf16[1024,8,2,128]{3,2,1,0:T(2,128)(2,1)} %param.7) | data formatting | bytes 8388608 | tf_op jit(solution)/shard_map/reshape | solution.py:89
  40.9 12.0 %convolution_convert_fusion = bf16[2048,2048]{0,1:T(8,128)(2,1)S(1)} fusion(bf16[2048,1024]{1,0:T(8,128)(2,1)} %param.6, bf16[1024,2048]{1,0:T(8,128)(2,1)} %reshape.111), kind=kOutput, calls=%fused_computation.3 | convolution fusion | flops 8594128896 | bytes 16777216 | tf_op jit(solution)/shard_map/dot_general | solution.py:90
  52.9 0.0 copy-start.1
  52.9 2.5 dynamic-slice_bitcast_fusion
  55.4 2.1 copy-done.1
  57.5 2.1 collective-permute-start
  59.7 7.1 %collective-permute-done = bf16[4,2048,256]{1,2,0:T(8,128)(2,1)} collective-permute-done((bf16[4,2048,256]{1,2,0:T(8,128)(2,1)}, bf16[4,2048,256]{1,2,0:T(8,128)(2,1)}, u32[]{:S(2)}, u32[]{:S(2)}) %collective-permute-start) | collective-permute-done | bytes 4194336 | tf_op jit(solution)/shard_map/ppermute | solution.py:57
  66.8 5.4 %convert_add_fusion = f32[4,2048,256]{1,2,0:T(8,128)S(1)} fusion(bf16[4,2048,256]{1,2,0:T(8,128)(2,1)} %collective-permute-done, bf16[4,2,2048,256]{2,3,1,0:T(8,128)(2,1)} %bitcast.39, s32[]{:T(128)S(6)} %select_n.154), kind=kLoop, calls=%fused_computation.2 | loop fusion | flops 6291456 | bytes 16777220 | tf_op jit(solution)/shard_map/add | solution.py:57
  72.2 3.9 %constant_dynamic-slice_fusion.2 = (f32[2,1,2048,256]{2,3,1,0:T(8,128)}, f32[2,1,2048,256]{2,3,1,0:T(8,128)}) fusion(f32[2,2,2048,256]{2,3,1,0:T(8,128)S(1)} %bitcast.37, s32[]{:T(128)S(6)} %select_n.158, s32[]{:T(128)S(6)} %select_n.159), kind=kLoop, calls=%fused_computation.48 | loop fusion | bytes 16777224 | tf_op jit(solution)/shard_map/jit(dynamic_index_in_dim)/dynamic_slice | solution.py:55
  76.0 5.4 %copy.19 = f32[2,1,2048,256]{3,2,0,1:T(8,128)} copy(f32[2,1,2048,256]{2,3,1,0:T(8,128)} %get-tuple-element.12) | data formatting | bytes 8388608
  81.4 1.2 collective-permute-start.1
  82.6 5.3 %copy.18 = f32[2,1,2048,256]{3,2,0,1:T(8,128)} copy(f32[2,1,2048,256]{2,3,1,0:T(8,128)} %get-tuple-element.11) | data formatting | bytes 8388608
  88.0 85.5 %collective-permute-done.1 = f32[2,2048,256]{2,1,0:T(8,128)} collective-permute-done((f32[2,2048,256]{2,1,0:T(8,128)}, f32[2,2048,256]{2,1,0:T(8,128)}, u32[]{:S(2)}, u32[]{:S(2)}) %collective-permute-start.1) | collective-permute-done | bytes 4194336 | tf_op jit(solution)/shard_map/ppermute | solution.py:57
  173.5 4.0 %bitcast_add_fusion = f32[2,2048,256]{2,1,0:T(8,128)S(1)} fusion(f32[2,2048,256]{2,1,0:T(8,128)} %collective-permute-done.1, f32[2,1,2048,256]{3,2,0,1:T(8,128)} %copy.18), kind=kLoop, calls=%fused_computation.6 | loop fusion | flops 1048576 | bytes 12582912 | tf_op jit(solution)/shard_map/add | solution.py:57
  177.5 0.0 copy-start
  177.5 2.0 copy-done
  179.5 0.1 constant_dynamic-slice_fusion
  179.7 2.8 collective-permute-start.2
  182.5 44.8 %collective-permute-done.2 = f32[1,2048,256]{2,1,0:T(8,128)} collective-permute-done((f32[1,2048,256]{2,1,0:T(8,128)S(1)}, f32[1,2048,256]{2,1,0:T(8,128)}, u32[]{:S(2)}, u32[]{:S(2)}) %collective-permute-start.2) | collective-permute-done | bytes 2097184 | tf_op jit(solution)/shard_map/ppermute | solution.py:57
  227.3 2.5 dynamic-slice_add_fusion
  229.8 19.0 %all-to-all-done.1 = bf16[32,1152,128]{2,1,0:T(8,128)(2,1)} async-done(((bf16[32,1152,128]{2,1,0:T(8,128)(2,1)}), bf16[32,1152,128]{2,1,0:T(8,128)(2,1)}, u32[]{:S(2)}, u32[]{:S(2)}) %all-to-all-start.1) | async-done | bytes 9437216 | tf_op jit(solution)/shard_map/all_to_all | solution.py:85
  248.8 7.1 %gather_fusion.1 = bf16[16,1152,128]{2,1,0:T(8,128)(2,1)} fusion(bf16[32,1152,128]{2,1,0:T(8,128)(2,1)} %all-to-all-done.1, s32[1024]{0:T(1024)S(1)} %pad_clamp_fusion), kind=kCustom, calls=%fused_computation.1 | custom fusion | bytes 9437248 | tf_op jit(solution)/shard_map/gather | solution.py:96
  255.9 4.7 %fusion.2 = f32[16,128,128]{2,1,0:T(8,128)S(1)} fusion(bf16[16,128,1024]{2,1,0:T(8,128)(2,1)} %bitcast.45, bf16[16,1152,128]{2,1,0:T(8,128)(2,1)} %gather_fusion.1), kind=kOutput, calls=%fused_computation.11 | convolution fusion | flops 536870912 | bytes 9437184 | tf_op jit(solution)/shard_map/rtd,rdc->rtc/dot_general | solution.py:100
  260.6 0.0 copy-start.2
  260.6 0.1 slice_select_fusion.1
  260.7 1.5 collective-permute-start.3
  262.2 1.7 collective-permute-done.3
  263.9 1.1 bitcast_add_fusion.2
  265.0 1.3 collective-permute-start.4
  266.3 6.3 %collective-permute-done.4 = f32[512,128]{1,0:T(8,128)S(1)} collective-permute-done((f32[512,128]{1,0:T(8,128)S(1)}, f32[512,128]{1,0:T(8,128)S(1)}, u32[]{:S(2)}, u32[]{:S(2)}) %collective-permute-start.4) | collective-permute-done | bytes 262176 | tf_op jit(solution)/shard_map/ppermute | solution.py:34
  272.6 2.8 collective-permute-start.5
  275.5 0.0 copy-done.2
  275.5 2.6 collective-permute-done.5
  278.1 2.8 collective-permute-start.6
  280.9 0.1 convert_bitcast_fusion
  281.0 1.8 collective-permute-done.6
  282.8 1.3 collective-permute-start.7
  284.1 3.0 collective-permute-done.7
  287.1 0.1 maximum_select_fusion.1
  287.2 4.4 %collective-permute-start.8 = (bf16[1024,128]{1,0:T(8,128)(2,1)S(1)}, bf16[1024,128]{1,0:T(8,128)(2,1)S(1)}, u32[]{:S(2)}, u32[]{:S(2)}) collective-permute-start(bf16[1024,128]{1,0:T(8,128)(2,1)S(1)} %maximum_select_fusion.1), channel_id=1, source_target_pairs={{0,1},{1,0},{2,3},{3,2},{4,5},{5,4},{6,7},{7,6},{8,9},{9,8},{10,11... | collective-permute-start | bytes 786440 | tf_op jit(solution)/shard_map/ppermute | solution.py:39
  291.6 1.2 broadcast_select_fusion.1
  292.8 0.0 collective-permute-done.8
  292.8 0.1 maximum_select_fusion
  292.9 0.4 fusion.7
  293.3 0.4 bitcast_add_fusion.1
  293.7 0.1 slice.100
  293.8 0.6 slice_negate_fusion
  294.4 4.7 %fusion.6 = bf16[2048,128]{1,0:T(8,128)(2,1)S(1)} fusion(f32[2048,256]{1,0:T(8,128)S(1)} %bitcast_add_fusion.1, f32[2048,64]{1,0:T(8,128)S(1)} %get-tuple-element.16, f32[2048,64]{1,0:T(8,128)S(1)} %get-tuple-element.15, f32[2048,64]{1,0:T(8,128)S(1)} %get-tuple-element.20), kind=kLoop, calls=%fused_computation.16 | loop fusion | flops 1572864 | bytes 3145728 | tf_op jit(solution)/shard_map/convert.1
  299.2 0.1 pad_maximum_fusion.2
  299.3 1.1 convert_element_type.43
  (11 shorter events, 0.2 us)
Async XLA Ops:
  1.4 20.6 %all-to-all-start = ((s32[32,1,1]{2,1,0:T(1,128)}), s32[32,1,1]{2,1,0:T(1,128)S(1)}, u32[]{:S(2)}, u32[]{:S(2)}) async-start(s32[32,1,1]{2,1,0:T(1,128)} %copy.15), calls=%async_computation | async-start | bytes 32768 | tf_op jit(solution)/shard_map/all_to_all | solution.py:78
  28.1 220.7 %all-to-all-start.1 = ((bf16[32,1152,128]{2,1,0:T(8,128)(2,1)}), bf16[32,1152,128]{2,1,0:T(8,128)(2,1)}, u32[]{:S(2)}, u32[]{:S(2)}) async-start(bf16[32,1152,128]{2,1,0:T(8,128)(2,1)} %gather_fusion), calls=%async_computation.1 | async-start | bytes 18874368 | tf_op jit(solution)/shard_map/all_to_all | solution.py:85
  52.9 4.7 %copy-start.1 = (bf16[2048,2048]{0,1:T(8,128)(2,1)}, bf16[2048,2048]{0,1:T(8,128)(2,1)S(1)}, u32[]{:S(2)}) copy-start(bf16[2048,2048]{0,1:T(8,128)(2,1)S(1)} %convolution_convert_fusion) | copy-start | bytes 25165828
  57.5 9.2 %collective-permute-start = (bf16[4,2048,256]{1,2,0:T(8,128)(2,1)}, bf16[4,2048,256]{1,2,0:T(8,128)(2,1)}, u32[]{:S(2)}, u32[]{:S(2)}) collective-permute-start(bf16[4,2048,256]{1,2,0:T(8,128)(2,1)} %dynamic-slice_bitcast_fusion), channel_id=1, source_target_pairs={{0,1},{1,0},{2,3},{3,2},{4,5},{5,4},{6,7},{7,6},{8,9},{9,8},{10,11... | collective-permute-start | bytes 12582920 | tf_op jit(solution)/shard_map/ppermute | solution.py:57
  81.4 92.1 %collective-permute-start.1 = (f32[2,2048,256]{2,1,0:T(8,128)}, f32[2,2048,256]{2,1,0:T(8,128)}, u32[]{:S(2)}, u32[]{:S(2)}) collective-permute-start(f32[2,2048,256]{2,1,0:T(8,128)} %bitcast.40), channel_id=1, source_target_pairs={{0,2},{1,3},{2,0},{3,1},{4,6},{5,7},{6,4},{7,5},{8,10},{9,11},{10,... | collective-permute-start | bytes 12582920 | tf_op jit(solution)/shard_map/ppermute | solution.py:57
  177.5 2.0 copy-start
  179.7 47.7 %collective-permute-start.2 = (f32[1,2048,256]{2,1,0:T(8,128)S(1)}, f32[1,2048,256]{2,1,0:T(8,128)}, u32[]{:S(2)}, u32[]{:S(2)}) collective-permute-start(f32[1,2048,256]{2,1,0:T(8,128)S(1)} %constant_dynamic-slice_fusion), channel_id=1, source_target_pairs={{0,4},{1,5},{2,6},{3,7},{4,0},{5,1},{6,2},{7,3},{8,12},{9,13},{10,... | collective-permute-start | bytes 6291464 | tf_op jit(solution)/shard_map/ppermute | solution.py:57
  260.6 14.9 %copy-start.2 = (s32[16]{0:T(128)S(1)}, s32[16]{0:T(128)}, u32[]{:S(2)}) copy-start(s32[16]{0:T(128)} %param.11) | copy-start | bytes 196
  260.7 3.2 %collective-permute-start.3 = (f32[1024,128]{1,0:T(8,128)S(1)}, f32[1024,128]{1,0:T(8,128)}, u32[]{:S(2)}, u32[]{:S(2)}) collective-permute-start(f32[1024,128]{1,0:T(8,128)S(1)} %bitcast.42), channel_id=1, source_target_pairs={{0,1},{1,0},{2,3},{3,2},{4,5},{5,4},{6,7},{7,6},{8,9},{9,8},{10,11... | collective-permute-start | bytes 1572872 | tf_op jit(solution)/shard_map/ppermute | solution.py:34
  265.0 7.6 %collective-permute-start.4 = (f32[512,128]{1,0:T(8,128)S(1)}, f32[512,128]{1,0:T(8,128)S(1)}, u32[]{:S(2)}, u32[]{:S(2)}) collective-permute-start(f32[512,128]{1,0:T(8,128)S(1)} %slice_select_fusion.2), channel_id=1, source_target_pairs={{0,2},{1,3},{2,0},{3,1},{4,6},{5,7},{6,4},{7,5},{8,10},{9,11},{10,... | collective-permute-start | bytes 786440 | tf_op jit(solution)/shard_map/ppermute | solution.py:34
  272.6 5.4 %collective-permute-start.5 = (f32[256,128]{1,0:T(8,128)S(1)}, f32[256,128]{1,0:T(8,128)S(1)}, u32[]{:S(2)}, u32[]{:S(2)}) collective-permute-start(f32[256,128]{1,0:T(8,128)S(1)} %slice_select_fusion.3), channel_id=1, source_target_pairs={{0,4},{1,5},{2,6},{3,7},{4,0},{5,1},{6,2},{7,3},{8,12},{9,13},{10,... | collective-permute-start | bytes 393224 | tf_op jit(solution)/shard_map/ppermute | solution.py:34
  278.1 4.7 %collective-permute-start.6 = (bf16[256,128]{1,0:T(8,128)(2,1)S(1)}, bf16[256,128]{1,0:T(8,128)(2,1)S(1)}, u32[]{:S(2)}, u32[]{:S(2)}) collective-permute-start(bf16[256,128]{1,0:T(8,128)(2,1)S(1)} %add_convert_fusion), channel_id=1, source_target_pairs={{0,4},{1,5},{2,6},{3,7},{4,0},{5,1},{6,2},{7,3},{8,12},{9,13},{10,... | collective-permute-start | bytes 196616 | tf_op jit(solution)/shard_map/ppermute | solution.py:39
  282.8 4.3 %collective-permute-start.7 = (bf16[512,128]{1,0:T(8,128)(2,1)S(1)}, bf16[512,128]{1,0:T(8,128)(2,1)S(1)}, u32[]{:S(2)}, u32[]{:S(2)}) collective-permute-start(bf16[512,128]{1,0:T(8,128)(2,1)S(1)} %maximum_select_fusion.2), channel_id=1, source_target_pairs={{0,2},{1,3},{2,0},{3,1},{4,6},{5,7},{6,4},{7,5},{8,10},{9,11},{10,... | collective-permute-start | bytes 393224 | tf_op jit(solution)/shard_map/ppermute | solution.py:39
  287.2 5.6 %collective-permute-start.8 = (bf16[1024,128]{1,0:T(8,128)(2,1)S(1)}, bf16[1024,128]{1,0:T(8,128)(2,1)S(1)}, u32[]{:S(2)}, u32[]{:S(2)}) collective-permute-start(bf16[1024,128]{1,0:T(8,128)(2,1)S(1)} %maximum_select_fusion.1), channel_id=1, source_target_pairs={{0,1},{1,0},{2,3},{3,2},{4,5},{5,4},{6,7},{7,6},{8,9},{9,8},{10,11... | collective-permute-start | bytes 786440 | tf_op jit(solution)/shard_map/ppermute | solution.py:39

commit v7 on v6

--- a/solution.py
+++ b/solution.py
@@ -25,15 +25,18 @@
         bits.append(bit)
         bit *= 2
     cur = v
-    for bit in bits:
+    for bit in bits[:-1]:
         half = cur.shape[0] // 2
         upper = (me & bit) > 0
         send = jnp.where(upper, cur[:half], cur[half:])
         keep = jnp.where(upper, cur[half:], cur[:half])
         pairs = [(i, i ^ bit) for i in range(count)]
         cur = keep + lax.ppermute(send, "narrow", pairs)
+    if bits:
+        pairs = [(i, i ^ bits[-1]) for i in range(count)]
+        cur = cur + lax.ppermute(cur, "narrow", pairs)
     cur = cur.astype(jnp.bfloat16)
-    for bit in reversed(bits):
+    for bit in reversed(bits[:-1]):
         upper = (me & bit) > 0
         pairs = [(i, i ^ bit) for i in range(count)]
         other = lax.ppermute(cur, "narrow", pairs)
@@ -93,7 +96,9 @@
     base_total_sum = narrow_scatter(partials)
     got, base_total_sum = lax.optimization_barrier((got, base_total_sum))
 
-    needed = got[owners]
+    needed = jnp.stack(
+        [lax.dynamic_index_in_dim(got, owners[r], keepdims=False) for r in range(requests)]
+    )
     needed_a = needed[:, :width]
     up = needed[:, width:]
     request_rows = hidden.reshape(requests, span_len, hidden.shape[1])

time: 301 us -> 305 us (1.013)
  waiting for transfers between devices: 178 us -> 147 us
  between operations: 0.22 us -> 30.1 us
  local copies, waits for them, and re-layouts: 43.6 us -> 55.6 us
  starting transfers between devices: 37.3 us -> 33.4 us
  matrix products: 17.1 us -> 13.6 us
    ppermute x3, waiting for transfers between devices: 137 us -> 107 us  [narrow_scatter(): lax.ppermute(theirs, 'narrow', pairs).astype(jnp.float32)]
    unnamed x8 -> x27, local copies, waits for them, and re-layouts: 14.9 us -> 32.4 us
    gather x1 -> x0, local copies, waits for them, and re-layouts: 7.06 us -> none  [shards(): needed = got[owners]]
    ppermute x0 -> x1, waiting for transfers between devices: none -> 5.32 us  [narrow_sum(): cur = cur + lax.ppermute(cur, 'narrow', pairs)]
    ppermute x3 -> x2, starting transfers between devices: 8.51 us -> 4.62 us  [narrow_sum(): other = lax.ppermute(cur, 'narrow', pairs)]
    dot_general x1, matrix products: 4.71 us -> 1.24 us  [shards(): jnp.einsum('rtd,rdc->rtc', request_rows, needed_a, preferred_element_type...]
    ppermute x3 -> x2, waiting for transfers between devices: 10.5 us -> 7.95 us  [narrow_sum(): cur = keep + lax.ppermute(send, 'narrow', pairs)]
  transfers between devices with their start and end apart: 11 -> 10, of which waited for: 10 -> 9; matrix products, arithmetic and copies ran while one was open for 17% -> 17% of each run, Pallas kernels for 0% -> 0%
where the time goes in v7:
time: 305 us; the launch traced here: 304 us
  waiting for transfers between devices  147 us (48%)
  local copies, waits for them, and re-layouts  55.6 us (18%)
  starting transfers between devices  33.4 us (11%)
  between operations  30.1 us (10%)
  other arithmetic  23.8 us (8%)
  matrix products  13.6 us (4%)
    ppermute x3, waiting for transfers between devices, narrow_scatter(): lax.ppermute(theirs, 'narrow', pairs).astype(jnp.float32)  107 us
    unnamed x27, local copies, waits for them, and re-layouts  32.4 us
    all_to_all x1, waiting for transfers between devices, shards(): got = lax.all_to_all(reply, 'wide', split_axis=0, concat_axis=0, tiled=True)  18 us
    all_to_all x1, starting transfers between devices, shards(): lax.all_to_all(wanted.reshape(wide_count, 1), 'wide', split_axis=0, conca...  12 us
    dot_general x1, matrix products, shards(): partials = jnp.dot(hidden, flat_w, preferred_element_type=jnp.float32)  12 us
    add x3, other arithmetic, narrow_scatter(): mine.astype(jnp.float32)  11.9 us
    ppermute x2, waiting for transfers between devices, narrow_sum(): cur = keep + lax.ppermute(send, 'narrow', pairs)  7.95 us
    reshape x1, local copies, waits for them, and re-layouts, shards(): flat_w = base_key_value.reshape(width, heads * 2 * head_size)  7.84 us
  transfers between devices with their start and end apart: 10, of which 9 were waited for; matrix products, arithmetic and copies ran while one was open for 17% of the time, Pallas kernels for 0%

profile of v7, /device:TPU:1, one launch (start us, length us, event | category | flops | bytes accessed | tf_op | source)
XLA Modules:
  0.0 303.9 jit_solution(12549927124297703712)
XLA Ops:
  0.0 0.7 and_select_fusion.1
  0.8 0.7 copy.15
  1.4 12.0 %all-to-all-start = ((s32[32,1,1]{2,1,0:T(1,128)}), s32[32,1,1]{2,1,0:T(1,128)S(1)}, u32[]{:S(2)}, u32[]{:S(2)}) async-start(s32[32,1,1]{2,1,0:T(1,128)} %copy.15), calls=%async_computation | async-start | bytes 32768 | tf_op jit(solution)/shard_map/all_to_all | solution.py:81
  13.5 1.9 pad_maximum_fusion
  15.3 6.7 %all-to-all-done = s32[32,1,1]{2,1,0:T(1,128)S(1)} async-done(((s32[32,1,1]{2,1,0:T(1,128)}), s32[32,1,1]{2,1,0:T(1,128)S(1)}, u32[]{:S(2)}, u32[]{:S(2)}) %all-to-all-start) | async-done | bytes 160 | tf_op jit(solution)/shard_map/all_to_all | solution.py:81
  22.0 0.7 reduce
  22.7 5.4 %gather_fusion = bf16[32,1152,128]{2,1,0:T(8,128)(2,1)} fusion(bf16[8,1152,128]{2,1,0:T(8,128)(2,1)S(1)} %pad_maximum_fusion, s32[1024]{0:T(1024)S(1)} %pad_clamp_fusion), kind=kCustom, calls=%fused_computation | custom fusion | bytes 18874496 | tf_op jit(solution)/shard_map/gather | solution.py:87
  28.1 5.0 %all-to-all-start.1 = ((bf16[32,1152,128]{2,1,0:T(8,128)(2,1)}), bf16[32,1152,128]{2,1,0:T(8,128)(2,1)}, u32[]{:S(2)}, u32[]{:S(2)}) async-start(bf16[32,1152,128]{2,1,0:T(8,128)(2,1)} %gather_fusion), calls=%async_computation.1 | async-start | bytes 18874368 | tf_op jit(solution)/shard_map/all_to_all | solution.py:88
  33.1 7.8 %reshape.111 = bf16[1024,2048]{1,0:T(8,128)(2,1)} reshape(bf16[1024,8,2,128]{3,2,1,0:T(2,128)(2,1)} %param.7) | data formatting | bytes 8388608 | tf_op jit(solution)/shard_map/reshape | solution.py:92
  40.9 12.0 %convolution_convert_fusion = bf16[2048,2048]{0,1:T(8,128)(2,1)S(1)} fusion(bf16[2048,1024]{1,0:T(8,128)(2,1)} %param.6, bf16[1024,2048]{1,0:T(8,128)(2,1)} %reshape.111), kind=kOutput, calls=%fused_computation.2 | convolution fusion | flops 8594128896 | bytes 16777216 | tf_op jit(solution)/shard_map/dot_general | solution.py:93
  52.9 3.4 %copy-done.1 = bf16[2048,2048]{0,1:T(8,128)(2,1)} copy-done((bf16[2048,2048]{0,1:T(8,128)(2,1)}, bf16[2048,2048]{0,1:T(8,128)(2,1)S(1)}, u32[]{:S(2)}) %copy-start.1) | copy-done | bytes 8388632
  56.3 2.2 dynamic-slice_bitcast_fusion
  58.5 2.1 collective-permute-start
  60.6 7.1 %collective-permute-done = bf16[4,2048,256]{1,2,0:T(8,128)(2,1)} collective-permute-done((bf16[4,2048,256]{1,2,0:T(8,128)(2,1)}, bf16[4,2048,256]{1,2,0:T(8,128)(2,1)}, u32[]{:S(2)}, u32[]{:S(2)}) %collective-permute-start) | collective-permute-done | bytes 4194336 | tf_op jit(solution)/shard_map/ppermute | solution.py:60
  67.8 5.4 %convert_add_fusion = f32[4,2048,256]{1,2,0:T(8,128)S(1)} fusion(bf16[4,2048,256]{1,2,0:T(8,128)(2,1)} %collective-permute-done, bf16[4,2,2048,256]{2,3,1,0:T(8,128)(2,1)} %bitcast.55, s32[]{:T(128)S(6)} %select_n.180), kind=kLoop, calls=%fused_computation.1 | loop fusion | flops 6291456 | bytes 16777220 | tf_op jit(solution)/shard_map/add | solution.py:60
  73.1 3.9 %constant_dynamic-slice_fusion.2 = (f32[2,1,2048,256]{2,3,1,0:T(8,128)}, f32[2,1,2048,256]{2,3,1,0:T(8,128)}) fusion(f32[2,2,2048,256]{2,3,1,0:T(8,128)S(1)} %bitcast.53, s32[]{:T(128)S(6)} %select_n.184, s32[]{:T(128)S(6)} %select_n.185), kind=kLoop, calls=%fused_computation.55 | loop fusion | bytes 16777224 | tf_op jit(solution)/shard_map/jit(dynamic_index_in_dim)/dynamic_slice | solution.py:58
  77.0 5.4 %copy.19 = f32[2,1,2048,256]{3,2,0,1:T(8,128)} copy(f32[2,1,2048,256]{2,3,1,0:T(8,128)} %get-tuple-element.10) | data formatting | bytes 8388608
  82.4 1.2 collective-permute-start.1
  83.6 5.4 %copy.18 = f32[2,1,2048,256]{3,2,0,1:T(8,128)} copy(f32[2,1,2048,256]{2,3,1,0:T(8,128)} %get-tuple-element.9) | data formatting | bytes 8388608
  89.0 85.5 %collective-permute-done.1 = f32[2,2048,256]{2,1,0:T(8,128)} collective-permute-done((f32[2,2048,256]{2,1,0:T(8,128)}, f32[2,2048,256]{2,1,0:T(8,128)}, u32[]{:S(2)}, u32[]{:S(2)}) %collective-permute-start.1) | collective-permute-done | bytes 4194336 | tf_op jit(solution)/shard_map/ppermute | solution.py:60
  174.5 4.0 %bitcast_add_fusion = f32[2,2048,256]{2,1,0:T(8,128)S(1)} fusion(f32[2,2048,256]{2,1,0:T(8,128)} %collective-permute-done.1, f32[2,1,2048,256]{3,2,0,1:T(8,128)} %copy.18), kind=kLoop, calls=%fused_computation.5 | loop fusion | flops 1048576 | bytes 12582912 | tf_op jit(solution)/shard_map/add | solution.py:60
  178.5 2.0 copy-done
  180.5 0.1 constant_dynamic-slice_fusion
  180.7 2.8 collective-permute-start.2
  183.5 0.7 fusion.13
  214.1 14.2 %collective-permute-done.2 = f32[1,2048,256]{2,1,0:T(8,128)} collective-permute-done((f32[1,2048,256]{2,1,0:T(8,128)S(1)}, f32[1,2048,256]{2,1,0:T(8,128)}, u32[]{:S(2)}, u32[]{:S(2)}) %collective-permute-start.2) | collective-permute-done | bytes 2097184 | tf_op jit(solution)/shard_map/ppermute | solution.py:60
  228.3 2.5 dynamic-slice_add_fusion
  230.8 18.0 %all-to-all-done.1 = bf16[32,1152,128]{2,1,0:T(8,128)(2,1)} async-done(((bf16[32,1152,128]{2,1,0:T(8,128)(2,1)}), bf16[32,1152,128]{2,1,0:T(8,128)(2,1)}, u32[]{:S(2)}, u32[]{:S(2)}) %all-to-all-start.1) | async-done | bytes 9437216 | tf_op jit(solution)/shard_map/all_to_all | solution.py:88
  248.8 1.1 dynamic-slice_dynamic-update-slice_fusion.15
  250.0 1.2 dynamic-slice_dynamic-update-slice_fusion.14
  251.2 1.0 dynamic-slice_dynamic-update-slice_fusion.13
  252.2 1.0 dynamic-slice_dynamic-update-slice_fusion.12
  253.2 1.0 dynamic-slice_dynamic-update-slice_fusion.11
  254.2 1.0 dynamic-slice_dynamic-update-slice_fusion.10
  255.2 1.0 dynamic-slice_dynamic-update-slice_fusion.9
  256.2 1.0 dynamic-slice_dynamic-update-slice_fusion.8
  257.2 1.0 dynamic-slice_dynamic-update-slice_fusion.7
  258.2 1.0 dynamic-slice_dynamic-update-slice_fusion.6
  259.2 1.0 dynamic-slice_dynamic-update-slice_fusion.5
  260.3 1.0 dynamic-slice_dynamic-update-slice_fusion.4
  261.3 1.0 dynamic-slice_dynamic-update-slice_fusion.3
  262.3 1.0 dynamic-slice_dynamic-update-slice_fusion.2
  263.3 1.0 dynamic-slice_dynamic-update-slice_fusion.1
  264.3 1.0 dynamic-slice_dynamic-update-slice_fusion
  265.3 1.2 fusion.2
  266.6 0.9 copy-done.2
  267.5 1.5 collective-permute-start.3
  269.0 1.7 collective-permute-done.3
  270.7 1.1 bitcast_add_fusion.2
  271.8 1.3 collective-permute-start.4
  273.1 6.3 %collective-permute-done.4 = f32[512,128]{1,0:T(8,128)S(1)} collective-permute-done((f32[512,128]{1,0:T(8,128)S(1)}, f32[512,128]{1,0:T(8,128)S(1)}, u32[]{:S(2)}, u32[]{:S(2)}) %collective-permute-start.4) | collective-permute-done | bytes 262176 | tf_op jit(solution)/shard_map/ppermute | solution.py:34
  279.5 2.8 collective-permute-start.5
  282.4 5.3 %collective-permute-done.5 = f32[512,128]{1,0:T(8,128)S(1)} collective-permute-done((f32[512,128]{1,0:T(8,128)S(1)}, f32[512,128]{1,0:T(8,128)S(1)}, u32[]{:S(2)}, u32[]{:S(2)}) %collective-permute-start.5) | collective-permute-done | bytes 262176 | tf_op jit(solution)/shard_map/ppermute | solution.py:37
  287.7 1.3 collective-permute-start.6
  289.0 2.6 collective-permute-done.6
  291.7 3.3 %collective-permute-start.7 = (bf16[1024,128]{1,0:T(8,128)(2,1)S(1)}, bf16[1024,128]{1,0:T(8,128)(2,1)S(1)}, u32[]{:S(2)}, u32[]{:S(2)}) collective-permute-start(bf16[1024,128]{1,0:T(8,128)(2,1)S(1)} %maximum_select_fusion.1), channel_id=1, source_target_pairs={{0,1},{1,0},{2,3},{3,2},{4,5},{5,4},{6,7},{7,6},{8,9},{9,8},{10,11... | collective-permute-start | bytes 786440 | tf_op jit(solution)/shard_map/ppermute | solution.py:42
  295.0 1.2 broadcast_select_fusion.1
  296.2 0.1 maximum_select_fusion
  296.4 0.4 fusion.7
  296.8 0.4 bitcast_add_fusion.1
  297.3 0.6 slice_negate_fusion
  297.9 4.7 %fusion.6 = bf16[2048,128]{1,0:T(8,128)(2,1)S(1)} fusion(f32[2048,256]{1,0:T(8,128)S(1)} %bitcast_add_fusion.1, f32[2048,64]{1,0:T(8,128)S(1)} %get-tuple-element.14, f32[2048,64]{1,0:T(8,128)S(1)} %get-tuple-element.13, f32[2048,64]{1,0:T(8,128)S(1)} %get-tuple-element.35), kind=kLoop, calls=%fused_computation.15 | loop fusion | flops 1572864 | bytes 3145728 | tf_op jit(solution)/shard_map/convert.1
  302.6 0.1 pad_maximum_fusion.2
  302.8 1.1 convert_element_type.43
  (21 shorter events, 0.5 us)
Async XLA Ops:
  1.4 20.6 %all-to-all-start = ((s32[32,1,1]{2,1,0:T(1,128)}), s32[32,1,1]{2,1,0:T(1,128)S(1)}, u32[]{:S(2)}, u32[]{:S(2)}) async-start(s32[32,1,1]{2,1,0:T(1,128)} %copy.15), calls=%async_computation | async-start | bytes 32768 | tf_op jit(solution)/shard_map/all_to_all | solution.py:81
  28.1 220.7 %all-to-all-start.1 = ((bf16[32,1152,128]{2,1,0:T(8,128)(2,1)}), bf16[32,1152,128]{2,1,0:T(8,128)(2,1)}, u32[]{:S(2)}, u32[]{:S(2)}) async-start(bf16[32,1152,128]{2,1,0:T(8,128)(2,1)} %gather_fusion), calls=%async_computation.1 | async-start | bytes 18874368 | tf_op jit(solution)/shard_map/all_to_all | solution.py:88
  52.9 3.4 %copy-start.1 = (bf16[2048,2048]{0,1:T(8,128)(2,1)}, bf16[2048,2048]{0,1:T(8,128)(2,1)S(1)}, u32[]{:S(2)}) copy-start(bf16[2048,2048]{0,1:T(8,128)(2,1)S(1)} %convolution_convert_fusion) | copy-start | bytes 25165828
  58.5 9.2 %collective-permute-start = (bf16[4,2048,256]{1,2,0:T(8,128)(2,1)}, bf16[4,2048,256]{1,2,0:T(8,128)(2,1)}, u32[]{:S(2)}, u32[]{:S(2)}) collective-permute-start(bf16[4,2048,256]{1,2,0:T(8,128)(2,1)} %dynamic-slice_bitcast_fusion), channel_id=1, source_target_pairs={{0,1},{1,0},{2,3},{3,2},{4,5},{5,4},{6,7},{7,6},{8,9},{9,8},{10,11... | collective-permute-start | bytes 12582920 | tf_op jit(solution)/shard_map/ppermute | solution.py:60
  82.4 92.1 %collective-permute-start.1 = (f32[2,2048,256]{2,1,0:T(8,128)}, f32[2,2048,256]{2,1,0:T(8,128)}, u32[]{:S(2)}, u32[]{:S(2)}) collective-permute-start(f32[2,2048,256]{2,1,0:T(8,128)} %bitcast.56), channel_id=1, source_target_pairs={{0,2},{1,3},{2,0},{3,1},{4,6},{5,7},{6,4},{7,5},{8,10},{9,11},{10,... | collective-permute-start | bytes 12582920 | tf_op jit(solution)/shard_map/ppermute | solution.py:60
  178.5 2.0 copy-start
  180.7 47.7 %collective-permute-start.2 = (f32[1,2048,256]{2,1,0:T(8,128)S(1)}, f32[1,2048,256]{2,1,0:T(8,128)}, u32[]{:S(2)}, u32[]{:S(2)}) collective-permute-start(f32[1,2048,256]{2,1,0:T(8,128)S(1)} %constant_dynamic-slice_fusion), channel_id=1, source_target_pairs={{0,4},{1,5},{2,6},{3,7},{4,0},{5,1},{6,2},{7,3},{8,12},{9,13},{10,... | collective-permute-start | bytes 6291464 | tf_op jit(solution)/shard_map/ppermute | solution.py:60
  248.8 16.5 %copy-start.3 = (bf16[2048,1024]{1,0:T(8,128)(2,1)S(1)}, bf16[2048,1024]{1,0:T(8,128)(2,1)}, u32[]{:S(2)}) copy-start(bf16[2048,1024]{1,0:T(8,128)(2,1)} %param.6) | copy-start | bytes 12582916
  265.3 2.1 copy-start.2
  267.4 14.9 %copy-start.4 = (s32[16]{0:T(128)S(1)}, s32[16]{0:T(128)}, u32[]{:S(2)}) copy-start(s32[16]{0:T(128)} %param.11) | copy-start | bytes 196
  267.5 3.2 %collective-permute-start.3 = (f32[1024,128]{1,0:T(8,128)S(1)}, f32[1024,128]{1,0:T(8,128)}, u32[]{:S(2)}, u32[]{:S(2)}) collective-permute-start(f32[1024,128]{1,0:T(8,128)S(1)} %bitcast.58), channel_id=1, source_target_pairs={{0,1},{1,0},{2,3},{3,2},{4,5},{5,4},{6,7},{7,6},{8,9},{9,8},{10,11... | collective-permute-start | bytes 1572872 | tf_op jit(solution)/shard_map/ppermute | solution.py:34
  271.8 7.6 %collective-permute-start.4 = (f32[512,128]{1,0:T(8,128)S(1)}, f32[512,128]{1,0:T(8,128)S(1)}, u32[]{:S(2)}, u32[]{:S(2)}) collective-permute-start(f32[512,128]{1,0:T(8,128)S(1)} %slice_select_fusion.2), channel_id=1, source_target_pairs={{0,2},{1,3},{2,0},{3,1},{4,6},{5,7},{6,4},{7,5},{8,10},{9,11},{10,... | collective-permute-start | bytes 786440 | tf_op jit(solution)/shard_map/ppermute | solution.py:34
  279.5 8.2 %collective-permute-start.5 = (f32[512,128]{1,0:T(8,128)S(1)}, f32[512,128]{1,0:T(8,128)S(1)}, u32[]{:S(2)}, u32[]{:S(2)}) collective-permute-start(f32[512,128]{1,0:T(8,128)S(1)} %select_add_fusion), channel_id=1, source_target_pairs={{0,4},{1,5},{2,6},{3,7},{4,0},{5,1},{6,2},{7,3},{8,12},{9,13},{10,... | collective-permute-start | bytes 786440 | tf_op jit(solution)/shard_map/ppermute | solution.py:37
  287.7 3.9 %collective-permute-start.6 = (bf16[512,128]{1,0:T(8,128)(2,1)S(1)}, bf16[512,128]{1,0:T(8,128)(2,1)S(1)}, u32[]{:S(2)}, u32[]{:S(2)}) collective-permute-start(bf16[512,128]{1,0:T(8,128)(2,1)S(1)} %add_convert_fusion), channel_id=1, source_target_pairs={{0,2},{1,3},{2,0},{3,1},{4,6},{5,7},{6,4},{7,5},{8,10},{9,11},{10,... | collective-permute-start | bytes 393224 | tf_op jit(solution)/shard_map/ppermute | solution.py:42
  291.7 4.5 %collective-permute-start.7 = (bf16[1024,128]{1,0:T(8,128)(2,1)S(1)}, bf16[1024,128]{1,0:T(8,128)(2,1)S(1)}, u32[]{:S(2)}, u32[]{:S(2)}) collective-permute-start(bf16[1024,128]{1,0:T(8,128)(2,1)S(1)} %maximum_select_fusion.1), channel_id=1, source_target_pairs={{0,1},{1,0},{2,3},{3,2},{4,5},{5,4},{6,7},{7,6},{8,9},{9,8},{10,11... | collective-permute-start | bytes 786440 | tf_op jit(solution)/shard_map/ppermute | solution.py:42

commit v8 on v7

--- a/solution.py
+++ b/solution.py
@@ -5,15 +5,6 @@
 
 
 THETA = 500000.0
-
-
-def rotate_keys(values, positions):
-    half_dim = values.shape[-1] // 2
-    frequency = THETA ** (-(jnp.arange(half_dim, dtype=jnp.float32) * 2.0 / values.shape[-1]))
-    angles = positions[:, None] * frequency[None, :]
-    angles = jnp.concatenate([angles, angles], axis=-1)
-    turned = jnp.concatenate([-values[..., half_dim:], values[..., :half_dim]], axis=-1)
-    return values * jnp.cos(angles) + turned * jnp.sin(angles)
 
 
 def narrow_sum(v):
@@ -94,11 +85,20 @@
     partials = partials.astype(jnp.bfloat16).reshape(tokens, heads, 2 * head_size)
     partials = partials.transpose(1, 0, 2)
     base_total_sum = narrow_scatter(partials)
-    got, base_total_sum = lax.optimization_barrier((got, base_total_sum))
+    positions = (
+        (span_start[:, None] * span_len + jnp.arange(span_len, dtype=jnp.int32)[None, :])
+        .reshape(-1)
+        .astype(jnp.float32)
+    )
+    half_dim = head_size // 2
+    frequency = THETA ** (-(jnp.arange(half_dim, dtype=jnp.float32) * 2.0 / head_size))
+    angles = positions[:, None] * frequency[None, :]
+    angles = jnp.concatenate([angles, angles], axis=-1)
+    got, base_total_sum, cos, sin = lax.optimization_barrier(
+        (got, base_total_sum, jnp.cos(angles), jnp.sin(angles))
+    )
 
-    needed = jnp.stack(
-        [lax.dynamic_index_in_dim(got, owners[r], keepdims=False) for r in range(requests)]
-    )
+    needed = got[owners]
     needed_a = needed[:, :width]
     up = needed[:, width:]
     request_rows = hidden.reshape(requests, span_len, hidden.shape[1])
@@ -118,12 +118,9 @@
         preferred_element_type=jnp.float32,
     ).reshape(tokens, 2 * head_size)
     raw = base_total_sum.reshape(tokens, 2 * head_size).astype(jnp.float32) + delta
-    positions = (
-        (span_start[:, None] * span_len + jnp.arange(span_len, dtype=jnp.int32)[None, :])
-        .reshape(-1)
-        .astype(jnp.float32)
-    )
-    keys_turned = rotate_keys(raw[:, :head_size], positions)
+    keys = raw[:, :head_size]
+    turned = jnp.concatenate([-keys[:, half_dim:], keys[:, :half_dim]], axis=-1)
+    keys_turned = keys * cos + turned * sin
     joined = jnp.concatenate([keys_turned, raw[:, head_size:]], axis=1)
     return joined.astype(jnp.bfloat16).reshape(base_total_sum.shape[0], tokens, 2, head_size)
 

time: 305 us -> 295 us (0.967)
  between operations: 30.1 us -> 0.24 us
  waiting for transfers between devices: 147 us -> 175 us
  local copies, waits for them, and re-layouts: 55.6 us -> 44.5 us
  matrix products: 13.6 us -> 17.1 us
    ppermute x3, waiting for transfers between devices: 107 us -> 132 us  [narrow_scatter(): lax.ppermute(theirs, 'narrow', pairs).astype(jnp.float32)]
    unnamed x27 -> x12, local copies, waits for them, and re-layouts: 32.4 us -> 15.7 us
    gather x0 -> x1, local copies, waits for them, and re-layouts: none -> 7.07 us  [shards(): needed = got[owners]]
    sin x0 -> x1, other arithmetic: none -> 4.74 us  [shards(): jnp.sin(angles)]
    another operation x1, other arithmetic: 4.74 us -> 0.43 us
    dot_general x1, matrix products: 1.24 us -> 4.71 us  [shards(): jnp.einsum('rtd,rdc->rtc', request_rows, needed_a, preferred_element_type...]
  transfers between devices with their start and end apart: 10 -> 10, of which waited for: 9 -> 9; matrix products, arithmetic and copies ran while one was open for 17% -> 19% of each run, Pallas kernels for 0% -> 0%
where the time goes in v8:
time: 295 us
  waiting for transfers between devices  175 us (59%)
  local copies, waits for them, and re-layouts  44.5 us (15%)
  starting transfers between devices  33.3 us (11%)
  other arithmetic  24.8 us (8%)
  matrix products  17.1 us (6%)
    ppermute x3, waiting for transfers between devices, narrow_scatter(): lax.ppermute(theirs, 'narrow', pairs).astype(jnp.float32)  132 us
    all_to_all x1, waiting for transfers between devices, shards(): got = lax.all_to_all(reply, 'wide', split_axis=0, concat_axis=0, tiled=True)  19.6 us
    unnamed x12, local copies, waits for them, and re-layouts  15.7 us
    all_to_all x1, starting transfers between devices, shards(): lax.all_to_all(wanted.reshape(wide_count, 1), 'wide', split_axis=0, conca...  12 us
    dot_general x1, matrix products, shards(): partials = jnp.dot(hidden, flat_w, preferred_element_type=jnp.float32)  12 us
    add x3, other arithmetic, narrow_scatter(): mine.astype(jnp.float32)  11.2 us
    ppermute x2, waiting for transfers between devices, narrow_sum(): cur = keep + lax.ppermute(send, 'narrow', pairs)  8.16 us
    reshape x1, local copies, waits for them, and re-layouts, shards(): flat_w = base_key_value.reshape(width, heads * 2 * head_size)  7.84 us
  transfers between devices with their start and end apart: 10, of which 9 were waited for; matrix products, arithmetic and copies ran while one was open for 19% of the time, Pallas kernels for 0%

profile of v8, /device:TPU:1, one launch (start us, length us, event | category | flops | bytes accessed | tf_op | source)
XLA Modules:
  0.0 294.6 jit_solution(14571117824284506658)
XLA Ops:
  0.0 0.7 compare_select_fusion
  0.7 0.1 select_reduce_fusion
  0.8 0.7 copy.15
  1.4 12.0 %all-to-all-start = ((s32[32,1,1]{2,1,0:T(1,128)}), s32[32,1,1]{2,1,0:T(1,128)S(1)}, u32[]{:S(2)}, u32[]{:S(2)}) async-start(s32[32,1,1]{2,1,0:T(1,128)} %copy.15), calls=%async_computation | async-start | bytes 32768 | tf_op jit(solution)/shard_map/all_to_all | solution.py:72
  13.5 1.9 pad_maximum_fusion
  15.3 6.7 %all-to-all-done = s32[32,1,1]{2,1,0:T(1,128)S(1)} async-done(((s32[32,1,1]{2,1,0:T(1,128)}), s32[32,1,1]{2,1,0:T(1,128)S(1)}, u32[]{:S(2)}, u32[]{:S(2)}) %all-to-all-start) | async-done | bytes 160 | tf_op jit(solution)/shard_map/all_to_all | solution.py:72
  22.0 0.7 reduce
  22.7 5.4 %gather_fusion = bf16[32,1152,128]{2,1,0:T(8,128)(2,1)} fusion(bf16[8,1152,128]{2,1,0:T(8,128)(2,1)S(1)} %pad_maximum_fusion, s32[1024]{0:T(1024)S(1)} %pad_clamp_fusion.1), kind=kCustom, calls=%fused_computation | custom fusion | bytes 18874496 | tf_op jit(solution)/shard_map/gather | solution.py:78
  28.1 5.0 %all-to-all-start.1 = ((bf16[32,1152,128]{2,1,0:T(8,128)(2,1)}), bf16[32,1152,128]{2,1,0:T(8,128)(2,1)}, u32[]{:S(2)}, u32[]{:S(2)}) async-start(bf16[32,1152,128]{2,1,0:T(8,128)(2,1)} %gather_fusion), calls=%async_computation.1 | async-start | bytes 18874368 | tf_op jit(solution)/shard_map/all_to_all | solution.py:79
  33.1 7.8 %reshape.111 = bf16[1024,2048]{1,0:T(8,128)(2,1)} reshape(bf16[1024,8,2,128]{3,2,1,0:T(2,128)(2,1)} %param.7) | data formatting | bytes 8388608 | tf_op jit(solution)/shard_map/reshape | solution.py:83
  40.9 12.0 %convolution_convert_fusion = bf16[2048,2048]{0,1:T(8,128)(2,1)S(1)} fusion(bf16[2048,1024]{1,0:T(8,128)(2,1)} %param.6, bf16[1024,2048]{1,0:T(8,128)(2,1)} %reshape.111), kind=kOutput, calls=%fused_computation.3 | convolution fusion | flops 8594128896 | bytes 16777216 | tf_op jit(solution)/shard_map/dot_general | solution.py:84
  52.9 0.0 copy-start.2
  52.9 2.5 dynamic-slice_bitcast_fusion
  55.5 2.1 copy-done.2
  57.6 2.1 collective-permute-start
  59.7 7.1 %collective-permute-done = bf16[4,2048,256]{1,2,0:T(8,128)(2,1)} collective-permute-done((bf16[4,2048,256]{1,2,0:T(8,128)(2,1)}, bf16[4,2048,256]{1,2,0:T(8,128)(2,1)}, u32[]{:S(2)}, u32[]{:S(2)}) %collective-permute-start) | collective-permute-done | bytes 4194336 | tf_op jit(solution)/shard_map/ppermute | solution.py:51
  66.8 5.4 %convert_add_fusion = f32[4,2048,256]{1,2,0:T(8,128)S(1)} fusion(bf16[4,2048,256]{1,2,0:T(8,128)(2,1)} %collective-permute-done, bf16[4,2,2048,256]{2,3,1,0:T(8,128)(2,1)} %bitcast.39, s32[]{:T(128)S(6)} %select_n.134), kind=kLoop, calls=%fused_computation.2 | loop fusion | flops 6291456 | bytes 16777220 | tf_op jit(solution)/shard_map/add | solution.py:51
  72.2 3.9 %constant_dynamic-slice_fusion.2 = (f32[2,1,2048,256]{2,3,1,0:T(8,128)}, f32[2,1,2048,256]{2,3,1,0:T(8,128)}) fusion(f32[2,2,2048,256]{2,3,1,0:T(8,128)S(1)} %bitcast.37, s32[]{:T(128)S(6)} %select_n.138, s32[]{:T(128)S(6)} %select_n.139), kind=kLoop, calls=%fused_computation.48 | loop fusion | bytes 16777224 | tf_op jit(solution)/shard_map/jit(dynamic_index_in_dim)/dynamic_slice | solution.py:49
  76.1 5.4 %copy.19 = f32[2,1,2048,256]{3,2,0,1:T(8,128)} copy(f32[2,1,2048,256]{2,3,1,0:T(8,128)} %get-tuple-element.16) | data formatting | bytes 8388608
  81.5 1.2 collective-permute-start.1
  82.7 5.4 %copy.18 = f32[2,1,2048,256]{3,2,0,1:T(8,128)} copy(f32[2,1,2048,256]{2,3,1,0:T(8,128)} %get-tuple-element.15) | data formatting | bytes 8388608
  88.1 85.5 %collective-permute-done.1 = f32[2,2048,256]{2,1,0:T(8,128)} collective-permute-done((f32[2,2048,256]{2,1,0:T(8,128)}, f32[2,2048,256]{2,1,0:T(8,128)}, u32[]{:S(2)}, u32[]{:S(2)}) %collective-permute-start.1) | collective-permute-done | bytes 4194336 | tf_op jit(solution)/shard_map/ppermute | solution.py:51
  173.6 4.0 %bitcast_add_fusion = f32[2,2048,256]{2,1,0:T(8,128)S(1)} fusion(f32[2,2048,256]{2,1,0:T(8,128)} %collective-permute-done.1, f32[2,1,2048,256]{3,2,0,1:T(8,128)} %copy.18), kind=kLoop, calls=%fused_computation.6 | loop fusion | flops 1048576 | bytes 12582912 | tf_op jit(solution)/shard_map/add | solution.py:51
  177.6 0.0 copy-start
  177.6 2.0 copy-done
  179.6 0.0 copy-start.4
  179.6 0.1 constant_dynamic-slice_fusion
  179.7 2.8 collective-permute-start.2
  182.6 0.0 copy-start.1
  182.6 0.0 copy-done.4
  182.6 0.1 convert_bitcast_fusion
  182.7 0.3 broadcast_multiply_fusion
  183.0 4.7 %fusion.11 = (f32[2048,128]{1,0:T(8,128)S(1)}, f32[2048,128]{1,0:T(8,128)}) fusion(f32[2048,64]{1,0:T(8,128)S(1)} %broadcast_multiply_fusion), kind=kLoop, calls=%fused_computation.24 | loop fusion | flops 262144 | bytes 2621440 | tf_op jit(solution)/shard_map/sin | solution.py:98
  187.8 39.6 %collective-permute-done.2 = f32[1,2048,256]{2,1,0:T(8,128)} collective-permute-done((f32[1,2048,256]{2,1,0:T(8,128)S(1)}, f32[1,2048,256]{2,1,0:T(8,128)}, u32[]{:S(2)}, u32[]{:S(2)}) %collective-permute-start.2) | collective-permute-done | bytes 2097184 | tf_op jit(solution)/shard_map/ppermute | solution.py:51
  227.4 0.0 copy-done.1
  227.4 1.9 dynamic-slice_add_fusion
  229.3 19.6 %all-to-all-done.1 = bf16[32,1152,128]{2,1,0:T(8,128)(2,1)} async-done(((bf16[32,1152,128]{2,1,0:T(8,128)(2,1)}), bf16[32,1152,128]{2,1,0:T(8,128)(2,1)}, u32[]{:S(2)}, u32[]{:S(2)}) %all-to-all-start.1) | async-done | bytes 9437216 | tf_op jit(solution)/shard_map/all_to_all | solution.py:79
  248.8 7.1 %gather_fusion.1 = bf16[16,1152,128]{2,1,0:T(8,128)(2,1)} fusion(bf16[32,1152,128]{2,1,0:T(8,128)(2,1)} %all-to-all-done.1, s32[1024]{0:T(1024)S(1)} %pad_clamp_fusion), kind=kCustom, calls=%fused_computation.1 | custom fusion | bytes 9437248 | tf_op jit(solution)/shard_map/gather | solution.py:101
  255.9 4.7 %fusion.2 = f32[16,128,128]{2,1,0:T(8,128)S(1)} fusion(bf16[16,128,1024]{2,1,0:T(8,128)(2,1)} %bitcast.44, bf16[16,1152,128]{2,1,0:T(8,128)(2,1)} %gather_fusion.1), kind=kOutput, calls=%fused_computation.11 | convolution fusion | flops 536870912 | bytes 9437184 | tf_op jit(solution)/shard_map/rtd,rdc->rtc/dot_general | solution.py:105
  260.6 1.1 slice_select_fusion.1
  261.7 1.4 collective-permute-start.3
  263.1 1.9 collective-permute-done.3
  265.0 1.3 bitcast_add_fusion.2
  266.3 1.3 collective-permute-start.4
  267.6 6.3 %collective-permute-done.4 = f32[512,128]{1,0:T(8,128)S(1)} collective-permute-done((f32[512,128]{1,0:T(8,128)S(1)}, f32[512,128]{1,0:T(8,128)S(1)}, u32[]{:S(2)}, u32[]{:S(2)}) %collective-permute-start.4) | collective-permute-done | bytes 262176 | tf_op jit(solution)/shard_map/ppermute | solution.py:25
  273.9 2.8 collective-permute-start.5
  276.7 5.4 %collective-permute-done.5 = f32[512,128]{1,0:T(8,128)S(1)} collective-permute-done((f32[512,128]{1,0:T(8,128)S(1)}, f32[512,128]{1,0:T(8,128)S(1)}, u32[]{:S(2)}, u32[]{:S(2)}) %collective-permute-start.5) | collective-permute-done | bytes 262176 | tf_op jit(solution)/shard_map/ppermute | solution.py:28
  282.2 1.3 collective-permute-start.6
  283.5 2.6 collective-permute-done.6
  286.1 0.1 maximum_select_fusion.1
  286.2 3.3 %collective-permute-start.7 = (bf16[1024,128]{1,0:T(8,128)(2,1)S(1)}, bf16[1024,128]{1,0:T(8,128)(2,1)S(1)}, u32[]{:S(2)}, u32[]{:S(2)}) collective-permute-start(bf16[1024,128]{1,0:T(8,128)(2,1)S(1)} %maximum_select_fusion.1), channel_id=1, source_target_pairs={{0,1},{1,0},{2,3},{3,2},{4,5},{5,4},{6,7},{7,6},{8,9},{9,8},{10,11... | collective-permute-start | bytes 786440 | tf_op jit(solution)/shard_map/ppermute | solution.py:33
  289.5 1.2 broadcast_select_fusion.1
  290.7 0.0 collective-permute-done.7
  290.7 0.1 maximum_select_fusion
  290.8 0.4 fusion.7
  291.3 0.4 bitcast_add_fusion.1
  291.7 0.0 copy-start.3
  291.7 0.3 slice_negate_fusion
  292.0 0.1 slice.84
  292.1 0.8 copy-done.3
  292.9 0.4 fusion.6
  293.3 0.1 pad_maximum_fusion.2
  293.4 1.1 convert_element_type.43
  (9 shorter events, 0.1 us)
Async XLA Ops:
  1.4 20.6 %all-to-all-start = ((s32[32,1,1]{2,1,0:T(1,128)}), s32[32,1,1]{2,1,0:T(1,128)S(1)}, u32[]{:S(2)}, u32[]{:S(2)}) async-start(s32[32,1,1]{2,1,0:T(1,128)} %copy.15), calls=%async_computation | async-start | bytes 32768 | tf_op jit(solution)/shard_map/all_to_all | solution.py:72
  28.1 220.7 %all-to-all-start.1 = ((bf16[32,1152,128]{2,1,0:T(8,128)(2,1)}), bf16[32,1152,128]{2,1,0:T(8,128)(2,1)}, u32[]{:S(2)}, u32[]{:S(2)}) async-start(bf16[32,1152,128]{2,1,0:T(8,128)(2,1)} %gather_fusion), calls=%async_computation.1 | async-start | bytes 18874368 | tf_op jit(solution)/shard_map/all_to_all | solution.py:79
  52.9 4.7 %copy-start.2 = (bf16[2048,2048]{0,1:T(8,128)(2,1)}, bf16[2048,2048]{0,1:T(8,128)(2,1)S(1)}, u32[]{:S(2)}) copy-start(bf16[2048,2048]{0,1:T(8,128)(2,1)S(1)} %convolution_convert_fusion) | copy-start | bytes 25165828
  57.6 9.2 %collective-permute-start = (bf16[4,2048,256]{1,2,0:T(8,128)(2,1)}, bf16[4,2048,256]{1,2,0:T(8,128)(2,1)}, u32[]{:S(2)}, u32[]{:S(2)}) collective-permute-start(bf16[4,2048,256]{1,2,0:T(8,128)(2,1)} %dynamic-slice_bitcast_fusion), channel_id=1, source_target_pairs={{0,1},{1,0},{2,3},{3,2},{4,5},{5,4},{6,7},{7,6},{8,9},{9,8},{10,11... | collective-permute-start | bytes 12582920 | tf_op jit(solution)/shard_map/ppermute | solution.py:51
  81.5 92.1 %collective-permute-start.1 = (f32[2,2048,256]{2,1,0:T(8,128)}, f32[2,2048,256]{2,1,0:T(8,128)}, u32[]{:S(2)}, u32[]{:S(2)}) collective-permute-start(f32[2,2048,256]{2,1,0:T(8,128)} %bitcast.40), channel_id=1, source_target_pairs={{0,2},{1,3},{2,0},{3,1},{4,6},{5,7},{6,4},{7,5},{8,10},{9,11},{10,... | collective-permute-start | bytes 12582920 | tf_op jit(solution)/shard_map/ppermute | solution.py:51
  177.6 2.0 copy-start
  179.6 3.0 %copy-start.4 = (s32[16]{0:T(128)S(1)}, s32[16]{0:T(128)}, u32[]{:S(2)}) copy-start(s32[16]{0:T(128)} %param.11) | copy-start | bytes 196
  179.7 47.7 %collective-permute-start.2 = (f32[1,2048,256]{2,1,0:T(8,128)S(1)}, f32[1,2048,256]{2,1,0:T(8,128)}, u32[]{:S(2)}, u32[]{:S(2)}) collective-permute-start(f32[1,2048,256]{2,1,0:T(8,128)S(1)} %constant_dynamic-slice_fusion), channel_id=1, source_target_pairs={{0,4},{1,5},{2,6},{3,7},{4,0},{5,1},{6,2},{7,3},{8,12},{9,13},{10,... | collective-permute-start | bytes 6291464 | tf_op jit(solution)/shard_map/ppermute | solution.py:51
  182.6 44.8 %copy-start.1 = (f32[2,2048,256]{2,1,0:T(8,128)S(1)}, f32[2,2048,256]{2,1,0:T(8,128)}, u32[]{:S(2)}) copy-start(f32[2,2048,256]{2,1,0:T(8,128)} %copy-done) | copy-start | bytes 12582916
  261.7 3.3 %collective-permute-start.3 = (f32[1024,128]{1,0:T(8,128)}, f32[1024,128]{1,0:T(8,128)}, u32[]{:S(2)}, u32[]{:S(2)}) collective-permute-start(f32[1024,128]{1,0:T(8,128)} %bitcast.18), channel_id=1, source_target_pairs={{0,1},{1,0},{2,3},{3,2},{4,5},{5,4},{6,7},{7,6},{8,9},{9,8},{10,11... | collective-permute-start | bytes 1572872 | tf_op jit(solution)/shard_map/ppermute | solution.py:25
  266.3 7.6 %collective-permute-start.4 = (f32[512,128]{1,0:T(8,128)S(1)}, f32[512,128]{1,0:T(8,128)S(1)}, u32[]{:S(2)}, u32[]{:S(2)}) collective-permute-start(f32[512,128]{1,0:T(8,128)S(1)} %slice_select_fusion.2), channel_id=1, source_target_pairs={{0,2},{1,3},{2,0},{3,1},{4,6},{5,7},{6,4},{7,5},{8,10},{9,11},{10,... | collective-permute-start | bytes 786440 | tf_op jit(solution)/shard_map/ppermute | solution.py:25
  273.9 8.2 %collective-permute-start.5 = (f32[512,128]{1,0:T(8,128)S(1)}, f32[512,128]{1,0:T(8,128)S(1)}, u32[]{:S(2)}, u32[]{:S(2)}) collective-permute-start(f32[512,128]{1,0:T(8,128)S(1)} %select_add_fusion), channel_id=1, source_target_pairs={{0,4},{1,5},{2,6},{3,7},{4,0},{5,1},{6,2},{7,3},{8,12},{9,13},{10,... | collective-permute-start | bytes 786440 | tf_op jit(solution)/shard_map/ppermute | solution.py:28
  282.2 3.9 %collective-permute-start.6 = (bf16[512,128]{1,0:T(8,128)(2,1)S(1)}, bf16[512,128]{1,0:T(8,128)(2,1)S(1)}, u32[]{:S(2)}, u32[]{:S(2)}) collective-permute-start(bf16[512,128]{1,0:T(8,128)(2,1)S(1)} %add_convert_fusion), channel_id=1, source_target_pairs={{0,2},{1,3},{2,0},{3,1},{4,6},{5,7},{6,4},{7,5},{8,10},{9,11},{10,... | collective-permute-start | bytes 393224 | tf_op jit(solution)/shard_map/ppermute | solution.py:33
  286.2 4.5 %collective-permute-start.7 = (bf16[1024,128]{1,0:T(8,128)(2,1)S(1)}, bf16[1024,128]{1,0:T(8,128)(2,1)S(1)}, u32[]{:S(2)}, u32[]{:S(2)}) collective-permute-start(bf16[1024,128]{1,0:T(8,128)(2,1)S(1)} %maximum_select_fusion.1), channel_id=1, source_target_pairs={{0,1},{1,0},{2,3},{3,2},{4,5},{5,4},{6,7},{7,6},{8,9},{9,8},{10,11... | collective-permute-start | bytes 786440 | tf_op jit(solution)/shard_map/ppermute | solution.py:33
  291.7 1.2 copy-start.3

commit v9 on v8

--- a/solution.py
+++ b/solution.py
@@ -18,9 +18,9 @@
     cur = v
     for bit in bits[:-1]:
         half = cur.shape[0] // 2
-        upper = (me & bit) > 0
-        send = jnp.where(upper, cur[:half], cur[half:])
-        keep = jnp.where(upper, cur[half:], cur[:half])
+        upper = (me // bit) % 2
+        send = lax.dynamic_slice_in_dim(cur, (1 - upper) * half, half)
+        keep = lax.dynamic_slice_in_dim(cur, upper * half, half)
         pairs = [(i, i ^ bit) for i in range(count)]
         cur = keep + lax.ppermute(send, "narrow", pairs)
     if bits:

time: 295 us -> 298 us (1.010)
    unnamed x12 -> x16, local copies, waits for them, and re-layouts: 15.7 us -> 17.5 us
where the time goes in v9:
time: 298 us; the launch traced here: 297 us
  waiting for transfers between devices  175 us (59%)
  local copies, waits for them, and re-layouts  47.1 us (16%)
  starting transfers between devices  33.3 us (11%)
  other arithmetic  24.7 us (8%)
  matrix products  17.1 us (6%)
    ppermute x3, waiting for transfers between devices, narrow_scatter(): lax.ppermute(theirs, 'narrow', pairs).astype(jnp.float32)  132 us
    all_to_all x1, waiting for transfers between devices, shards(): got = lax.all_to_all(reply, 'wide', split_axis=0, concat_axis=0, tiled=True)  19.6 us
    unnamed x16, local copies, waits for them, and re-layouts  17.5 us
    all_to_all x1, starting transfers between devices, shards(): lax.all_to_all(wanted.reshape(wide_count, 1), 'wide', split_axis=0, conca...  12 us
    dot_general x1, matrix products, shards(): partials = jnp.dot(hidden, flat_w, preferred_element_type=jnp.float32)  12 us
    add x3, other arithmetic, narrow_scatter(): mine.astype(jnp.float32)  11.2 us
    ppermute x2, waiting for transfers between devices, narrow_sum(): cur = keep + lax.ppermute(send, 'narrow', pairs)  8.26 us
    reshape x1, local copies, waits for them, and re-layouts, shards(): flat_w = base_key_value.reshape(width, heads * 2 * head_size)  7.83 us
  transfers between devices with their start and end apart: 10, of which 9 were waited for; matrix products, arithmetic and copies ran while one was open for 19% of the time, Pallas kernels for 0%

profile of v9, /device:TPU:1, one launch (start us, length us, event | category | flops | bytes accessed | tf_op | source)
XLA Modules:
  0.0 297.2 jit_solution(5474473406735687023)
XLA Ops:
  0.0 0.7 compare_select_fusion
  0.7 0.1 select_reduce_fusion
  0.8 0.7 copy.15
  1.4 12.0 %all-to-all-start = ((s32[32,1,1]{2,1,0:T(1,128)}), s32[32,1,1]{2,1,0:T(1,128)S(1)}, u32[]{:S(2)}, u32[]{:S(2)}) async-start(s32[32,1,1]{2,1,0:T(1,128)} %copy.15), calls=%async_computation | async-start | bytes 32768 | tf_op jit(solution)/shard_map/all_to_all | solution.py:72
  13.5 1.9 pad_maximum_fusion
  15.3 6.7 %all-to-all-done = s32[32,1,1]{2,1,0:T(1,128)S(1)} async-done(((s32[32,1,1]{2,1,0:T(1,128)}), s32[32,1,1]{2,1,0:T(1,128)S(1)}, u32[]{:S(2)}, u32[]{:S(2)}) %all-to-all-start) | async-done | bytes 160 | tf_op jit(solution)/shard_map/all_to_all | solution.py:72
  22.0 0.7 reduce
  22.7 5.4 %gather_fusion = bf16[32,1152,128]{2,1,0:T(8,128)(2,1)} fusion(bf16[8,1152,128]{2,1,0:T(8,128)(2,1)S(1)} %pad_maximum_fusion, s32[1024]{0:T(1024)S(1)} %pad_clamp_fusion.1), kind=kCustom, calls=%fused_computation | custom fusion | bytes 18874496 | tf_op jit(solution)/shard_map/gather | solution.py:78
  28.1 5.0 %all-to-all-start.1 = ((bf16[32,1152,128]{2,1,0:T(8,128)(2,1)}), bf16[32,1152,128]{2,1,0:T(8,128)(2,1)}, u32[]{:S(2)}, u32[]{:S(2)}) async-start(bf16[32,1152,128]{2,1,0:T(8,128)(2,1)} %gather_fusion), calls=%async_computation.1 | async-start | bytes 18874368 | tf_op jit(solution)/shard_map/all_to_all | solution.py:79
  33.1 7.8 %reshape.107 = bf16[1024,2048]{1,0:T(8,128)(2,1)} reshape(bf16[1024,8,2,128]{3,2,1,0:T(2,128)(2,1)} %param.7) | data formatting | bytes 8388608 | tf_op jit(solution)/shard_map/reshape | solution.py:83
  40.9 12.0 %convolution_convert_fusion = bf16[2048,2048]{0,1:T(8,128)(2,1)S(1)} fusion(bf16[2048,1024]{1,0:T(8,128)(2,1)} %param.6, bf16[1024,2048]{1,0:T(8,128)(2,1)} %reshape.107), kind=kOutput, calls=%fused_computation.3 | convolution fusion | flops 8594128896 | bytes 16777216 | tf_op jit(solution)/shard_map/dot_general | solution.py:84
  52.9 0.0 copy-start.2
  52.9 2.5 dynamic-slice_bitcast_fusion
  55.4 2.1 copy-done.2
  57.6 2.1 collective-permute-start
  59.7 7.1 %collective-permute-done = bf16[4,2048,256]{1,2,0:T(8,128)(2,1)} collective-permute-done((bf16[4,2048,256]{1,2,0:T(8,128)(2,1)}, bf16[4,2048,256]{1,2,0:T(8,128)(2,1)}, u32[]{:S(2)}, u32[]{:S(2)}) %collective-permute-start) | collective-permute-done | bytes 4194336 | tf_op jit(solution)/shard_map/ppermute | solution.py:51
  66.8 5.4 %convert_add_fusion = f32[4,2048,256]{1,2,0:T(8,128)S(1)} fusion(bf16[4,2048,256]{1,2,0:T(8,128)(2,1)} %collective-permute-done, bf16[4,2,2048,256]{2,3,1,0:T(8,128)(2,1)} %bitcast.37, s32[]{:T(128)S(6)} %select_n.122), kind=kLoop, calls=%fused_computation.2 | loop fusion | flops 6291456 | bytes 16777220 | tf_op jit(solution)/shard_map/add | solution.py:51
  72.2 3.9 %constant_dynamic-slice_fusion.4 = (f32[2,1,2048,256]{2,3,1,0:T(8,128)}, f32[2,1,2048,256]{2,3,1,0:T(8,128)}) fusion(f32[2,2,2048,256]{2,3,1,0:T(8,128)S(1)} %bitcast.35, s32[]{:T(128)S(6)} %select_n.126, s32[]{:T(128)S(6)} %select_n.127), kind=kLoop, calls=%fused_computation.44 | loop fusion | bytes 16777224 | tf_op jit(solution)/shard_map/jit(dynamic_index_in_dim)/dynamic_slice | solution.py:49
  76.1 5.4 %copy.19 = f32[2,1,2048,256]{3,2,0,1:T(8,128)} copy(f32[2,1,2048,256]{2,3,1,0:T(8,128)} %get-tuple-element.16) | data formatting | bytes 8388608
  81.5 1.2 collective-permute-start.1
  82.7 5.4 %copy.18 = f32[2,1,2048,256]{3,2,0,1:T(8,128)} copy(f32[2,1,2048,256]{2,3,1,0:T(8,128)} %get-tuple-element.15) | data formatting | bytes 8388608
  88.1 85.5 %collective-permute-done.1 = f32[2,2048,256]{2,1,0:T(8,128)} collective-permute-done((f32[2,2048,256]{2,1,0:T(8,128)}, f32[2,2048,256]{2,1,0:T(8,128)}, u32[]{:S(2)}, u32[]{:S(2)}) %collective-permute-start.1) | collective-permute-done | bytes 4194336 | tf_op jit(solution)/shard_map/ppermute | solution.py:51
  173.6 4.0 %bitcast_add_fusion = f32[2,2048,256]{2,1,0:T(8,128)S(1)} fusion(f32[2,2048,256]{2,1,0:T(8,128)} %collective-permute-done.1, f32[2,1,2048,256]{3,2,0,1:T(8,128)} %copy.18), kind=kLoop, calls=%fused_computation.6 | loop fusion | flops 1048576 | bytes 12582912 | tf_op jit(solution)/shard_map/add | solution.py:51
  177.6 0.0 copy-start
  177.6 2.0 copy-done
  179.6 0.1 constant_dynamic-slice_fusion.2
  179.7 2.8 collective-permute-start.2
  182.6 0.0 copy-done.6
  182.6 0.1 convert_bitcast_fusion
  182.7 0.3 broadcast_multiply_fusion
  183.0 4.7 %fusion.8 = (f32[2048,128]{1,0:T(8,128)S(1)}, f32[2048,128]{1,0:T(8,128)}) fusion(f32[2048,64]{1,0:T(8,128)S(1)} %broadcast_multiply_fusion), kind=kLoop, calls=%fused_computation.23 | loop fusion | flops 262144 | bytes 2621440 | tf_op jit(solution)/shard_map/sin | solution.py:98
  187.8 39.6 %collective-permute-done.2 = f32[1,2048,256]{2,1,0:T(8,128)} collective-permute-done((f32[1,2048,256]{2,1,0:T(8,128)S(1)}, f32[1,2048,256]{2,1,0:T(8,128)}, u32[]{:S(2)}, u32[]{:S(2)}) %collective-permute-start.2) | collective-permute-done | bytes 2097184 | tf_op jit(solution)/shard_map/ppermute | solution.py:51
  227.4 1.9 dynamic-slice_add_fusion
  229.3 19.6 %all-to-all-done.1 = bf16[32,1152,128]{2,1,0:T(8,128)(2,1)} async-done(((bf16[32,1152,128]{2,1,0:T(8,128)(2,1)}), bf16[32,1152,128]{2,1,0:T(8,128)(2,1)}, u32[]{:S(2)}, u32[]{:S(2)}) %all-to-all-start.1) | async-done | bytes 9437216 | tf_op jit(solution)/shard_map/all_to_all | solution.py:79
  248.8 7.1 %gather_fusion.1 = bf16[16,1152,128]{2,1,0:T(8,128)(2,1)} fusion(bf16[32,1152,128]{2,1,0:T(8,128)(2,1)} %all-to-all-done.1, s32[1024]{0:T(1024)S(1)} %pad_clamp_fusion), kind=kCustom, calls=%fused_computation.1 | custom fusion | bytes 9437248 | tf_op jit(solution)/shard_map/gather | solution.py:101
  255.9 4.7 %fusion = f32[16,128,128]{1,2,0:T(8,128)S(1)} fusion(bf16[16,128,1024]{2,1,0:T(8,128)(2,1)} %bitcast.44, bf16[16,1152,128]{2,1,0:T(8,128)(2,1)} %gather_fusion.1), kind=kOutput, calls=%fused_computation.4 | convolution fusion | flops 536870912 | bytes 9437184 | tf_op jit(solution)/shard_map/rtd,rdc->rtc/dot_general | solution.py:105
  260.6 0.0 copy-start.5
  260.6 1.0 copy-done.5
  261.6 0.8 constant_dynamic-slice_fusion.1
  262.4 1.4 collective-permute-start.3
  263.8 1.9 collective-permute-done.3
  265.7 1.3 dynamic-slice_add_fusion.1
  267.0 0.0 copy-start.4
  267.0 0.8 copy-done.4
  267.8 1.3 collective-permute-start.4
  269.1 6.4 %collective-permute-done.4 = f32[512,128]{1,0:T(8,128)} collective-permute-done((f32[512,128]{1,0:T(8,128)S(1)}, f32[512,128]{1,0:T(8,128)}, u32[]{:S(2)}, u32[]{:S(2)}) %collective-permute-start.4) | collective-permute-done | bytes 262176 | tf_op jit(solution)/shard_map/ppermute | solution.py:25
  275.5 1.1 dynamic-slice_add_fusion.2
  276.5 2.8 collective-permute-start.5
  279.4 5.4 %collective-permute-done.5 = f32[512,128]{1,0:T(8,128)S(1)} collective-permute-done((f32[512,128]{1,0:T(8,128)S(1)}, f32[512,128]{1,0:T(8,128)S(1)}, u32[]{:S(2)}, u32[]{:S(2)}) %collective-permute-start.5) | collective-permute-done | bytes 262176 | tf_op jit(solution)/shard_map/ppermute | solution.py:28
  284.8 1.3 collective-permute-start.6
  286.1 2.6 collective-permute-done.6
  288.7 0.1 maximum_select_fusion.1
  288.8 3.3 %collective-permute-start.7 = (bf16[1024,128]{1,0:T(8,128)(2,1)S(1)}, bf16[1024,128]{1,0:T(8,128)(2,1)S(1)}, u32[]{:S(2)}, u32[]{:S(2)}) collective-permute-start(bf16[1024,128]{1,0:T(8,128)(2,1)S(1)} %maximum_select_fusion.1), channel_id=1, source_target_pairs={{0,1},{1,0},{2,3},{3,2},{4,5},{5,4},{6,7},{7,6},{8,9},{9,8},{10,11... | collective-permute-start | bytes 786440 | tf_op jit(solution)/shard_map/ppermute | solution.py:33
  292.1 1.2 broadcast_select_fusion.1
  293.3 0.0 collective-permute-done.7
  293.3 0.1 maximum_select_fusion
  293.5 0.4 fusion.4
  293.9 0.4 bitcast_add_fusion.1
  294.3 0.3 slice_negate_fusion
  294.6 0.1 slice.48
  294.7 0.8 copy-done.3
  295.5 0.4 fusion.3
  295.9 0.1 pad_maximum_fusion.2
  296.1 1.1 convert_element_type.43
  (12 shorter events, 0.1 us)
Async XLA Ops:
  1.4 20.6 %all-to-all-start = ((s32[32,1,1]{2,1,0:T(1,128)}), s32[32,1,1]{2,1,0:T(1,128)S(1)}, u32[]{:S(2)}, u32[]{:S(2)}) async-start(s32[32,1,1]{2,1,0:T(1,128)} %copy.15), calls=%async_computation | async-start | bytes 32768 | tf_op jit(solution)/shard_map/all_to_all | solution.py:72
  28.1 220.7 %all-to-all-start.1 = ((bf16[32,1152,128]{2,1,0:T(8,128)(2,1)}), bf16[32,1152,128]{2,1,0:T(8,128)(2,1)}, u32[]{:S(2)}, u32[]{:S(2)}) async-start(bf16[32,1152,128]{2,1,0:T(8,128)(2,1)} %gather_fusion), calls=%async_computation.1 | async-start | bytes 18874368 | tf_op jit(solution)/shard_map/all_to_all | solution.py:79
  52.9 4.7 %copy-start.2 = (bf16[2048,2048]{0,1:T(8,128)(2,1)}, bf16[2048,2048]{0,1:T(8,128)(2,1)S(1)}, u32[]{:S(2)}) copy-start(bf16[2048,2048]{0,1:T(8,128)(2,1)S(1)} %convolution_convert_fusion) | copy-start | bytes 25165828
  57.6 9.2 %collective-permute-start = (bf16[4,2048,256]{1,2,0:T(8,128)(2,1)}, bf16[4,2048,256]{1,2,0:T(8,128)(2,1)}, u32[]{:S(2)}, u32[]{:S(2)}) collective-permute-start(bf16[4,2048,256]{1,2,0:T(8,128)(2,1)} %dynamic-slice_bitcast_fusion), channel_id=1, source_target_pairs={{0,1},{1,0},{2,3},{3,2},{4,5},{5,4},{6,7},{7,6},{8,9},{9,8},{10,11... | collective-permute-start | bytes 12582920 | tf_op jit(solution)/shard_map/ppermute | solution.py:51
  81.5 92.1 %collective-permute-start.1 = (f32[2,2048,256]{2,1,0:T(8,128)}, f32[2,2048,256]{2,1,0:T(8,128)}, u32[]{:S(2)}, u32[]{:S(2)}) collective-permute-start(f32[2,2048,256]{2,1,0:T(8,128)} %bitcast.38), channel_id=1, source_target_pairs={{0,2},{1,3},{2,0},{3,1},{4,6},{5,7},{6,4},{7,5},{8,10},{9,11},{10,... | collective-permute-start | bytes 12582920 | tf_op jit(solution)/shard_map/ppermute | solution.py:51
  177.6 2.0 copy-start
  179.6 3.0 %copy-start.6 = (s32[16]{0:T(128)S(1)}, s32[16]{0:T(128)}, u32[]{:S(2)}) copy-start(s32[16]{0:T(128)} %param.11) | copy-start | bytes 196
  179.7 47.7 %collective-permute-start.2 = (f32[1,2048,256]{2,1,0:T(8,128)S(1)}, f32[1,2048,256]{2,1,0:T(8,128)}, u32[]{:S(2)}, u32[]{:S(2)}) collective-permute-start(f32[1,2048,256]{2,1,0:T(8,128)S(1)} %constant_dynamic-slice_fusion.2), channel_id=1, source_target_pairs={{0,4},{1,5},{2,6},{3,7},{4,0},{5,1},{6,2},{7,3},{8,12},{9,13},{10,... | collective-permute-start | bytes 6291464 | tf_op jit(solution)/shard_map/ppermute | solution.py:51
  182.6 44.8 %copy-start.1 = (f32[2,2048,256]{2,1,0:T(8,128)S(1)}, f32[2,2048,256]{2,1,0:T(8,128)}, u32[]{:S(2)}) copy-start(f32[2,2048,256]{2,1,0:T(8,128)} %copy-done) | copy-start | bytes 12582916
  260.6 1.0 copy-start.5
  262.4 3.3 %collective-permute-start.3 = (f32[1024,128]{1,0:T(8,128)}, f32[1024,128]{1,0:T(8,128)}, u32[]{:S(2)}, u32[]{:S(2)}) collective-permute-start(f32[1024,128]{1,0:T(8,128)} %constant_dynamic-slice_fusion.1), channel_id=1, source_target_pairs={{0,1},{1,0},{2,3},{3,2},{4,5},{5,4},{6,7},{7,6},{8,9},{9,8},{10,11... | collective-permute-start | bytes 1572872 | tf_op jit(solution)/shard_map/ppermute | solution.py:25
  267.0 0.8 copy-start.4
  267.8 7.7 %collective-permute-start.4 = (f32[512,128]{1,0:T(8,128)S(1)}, f32[512,128]{1,0:T(8,128)}, u32[]{:S(2)}, u32[]{:S(2)}) collective-permute-start(f32[512,128]{1,0:T(8,128)S(1)} %constant_dynamic-slice_fusion), channel_id=1, source_target_pairs={{0,2},{1,3},{2,0},{3,1},{4,6},{5,7},{6,4},{7,5},{8,10},{9,11},{10,... | collective-permute-start | bytes 786440 | tf_op jit(solution)/shard_map/ppermute | solution.py:25
  276.5 8.2 %collective-permute-start.5 = (f32[512,128]{1,0:T(8,128)S(1)}, f32[512,128]{1,0:T(8,128)S(1)}, u32[]{:S(2)}, u32[]{:S(2)}) collective-permute-start(f32[512,128]{1,0:T(8,128)S(1)} %dynamic-slice_add_fusion.2), channel_id=1, source_target_pairs={{0,4},{1,5},{2,6},{3,7},{4,0},{5,1},{6,2},{7,3},{8,12},{9,13},{10,... | collective-permute-start | bytes 786440 | tf_op jit(solution)/shard_map/ppermute | solution.py:28
  284.8 3.9 %collective-permute-start.6 = (bf16[512,128]{1,0:T(8,128)(2,1)S(1)}, bf16[512,128]{1,0:T(8,128)(2,1)S(1)}, u32[]{:S(2)}, u32[]{:S(2)}) collective-permute-start(bf16[512,128]{1,0:T(8,128)(2,1)S(1)} %add_convert_fusion), channel_id=1, source_target_pairs={{0,2},{1,3},{2,0},{3,1},{4,6},{5,7},{6,4},{7,5},{8,10},{9,11},{10,... | collective-permute-start | bytes 393224 | tf_op jit(solution)/shard_map/ppermute | solution.py:33
  288.8 4.5 %collective-permute-start.7 = (bf16[1024,128]{1,0:T(8,128)(2,1)S(1)}, bf16[1024,128]{1,0:T(8,128)(2,1)S(1)}, u32[]{:S(2)}, u32[]{:S(2)}) collective-permute-start(bf16[1024,128]{1,0:T(8,128)(2,1)S(1)} %maximum_select_fusion.1), channel_id=1, source_target_pairs={{0,1},{1,0},{2,3},{3,2},{4,5},{5,4},{6,7},{7,6},{8,9},{9,8},{10,11... | collective-permute-start | bytes 786440 | tf_op jit(solution)/shard_map/ppermute | solution.py:33
  294.3 1.2 copy-start.3
